TPU v7x, 32 devices: a whole 2x2x4 slice. The times are simulated.
32 devices in a mesh: parts: 2 (over y), req: 8 (over z, x), mp: 2 (over core).
Axes of the slice: x: 2, y: 2, z: 4, core: 2. Of those that a mesh axis runs over, the one named last changes fastest.
Arguments:
- hidden: bfloat16 [2048, 8192], P(('parts', 'req'), 'mp'), parts along dimension 0, may hold values from -6 to 6
- base_query_block: bfloat16 [2048, 1024], P(('parts', 'req'), 'mp'), parts along dimension 0, may hold values from -112 to 112
- key_value_block: bfloat16 [2048, 256], P(('parts', 'req')), parts along dimension 0, may hold values from -7.1875 to 7.1875
- prefix_page_store: bfloat16 [256, 32, 256], P(('parts', 'req')), parts along dimension 0, may hold values from -8 to 8
- adapter_down_weight: bfloat16 [8, 2, 64, 4096], P('req', 'mp'), may hold values from -0.0625 to 0.0625
- adapter_up_weight: bfloat16 [8, 2, 64, 512], P('req', 'mp'), may hold values from -0.75 to 0.75
- request_adapter: int32 [16], P(('parts', 'req')), parts along dimension 0, may hold values from 0 to 7
- prefix_page_count: int32 [16], P(('parts', 'req')), parts along dimension 0, may hold values from 2 to 8, as said below
- page_owner_groups: int32 [16, 8], P(('parts', 'req')), parts along dimension 0, may hold values from 0 to 7, as said below
- page_pool_row: int32 [16, 8], P(('parts', 'req')), parts along dimension 0, may hold values from 0 to 15
Outputs:
- attn_out: bfloat16 [2048, 1024], P(('parts', 'req'), 'mp'), parts along dimension 0
There are 2 independent parts, one for each index of `parts`. A program takes and returns all parts, laid end to end along the dimension named above; an argument that names none is the same for every part. Nothing has to cross between parts.
Inputs may be any that keep to these rules, and one draw needn't show every extreme that they name: `prefix_page_count`: some request has exactly 8 prefix pages. `page_owner_groups`: each row names every request group once; its first prefix_page_count[r] entries hold request r's prefix pages, the rest is padding.
All inputs are finite; a program needn't handle non-finite values.
Results may differ from a plain program's by a relative error of at most 0.025.
Values may be sent and summed in bfloat16 or wider, within the bound.
No kernel may reach another device: no remote copies, remote signals or barrier semaphores. Data moves between devices by JAX's collectives and lax.ppermute only.
A program may use at most 64 MiB of HBM per device.

v0:
```python
import math

import jax
import jax.numpy as jnp
from jax import lax
from jax.sharding import PartitionSpec as P

ROPE_BASE = 500000.0


def rotate(vectors, positions):
    head_width = vectors.shape[-1]
    half_dim = head_width // 2
    frequency = ROPE_BASE ** (-2.0 * jnp.arange(half_dim, dtype=jnp.float32) / head_width)
    angles = positions.astype(jnp.float32)[:, None] * frequency[None, :]
    cosine = jnp.concatenate([jnp.cos(angles), jnp.cos(angles)], axis=1)[:, None, :]
    sine_part = jnp.concatenate([jnp.sin(angles), jnp.sin(angles)], axis=1)[:, None, :]
    turned = jnp.concatenate([-vectors[..., half_dim:], vectors[..., :half_dim]], axis=-1)
    return vectors * cosine + turned * sine_part


def attend(queries, all_keys, all_values, allowed):
    score_scale = 1.0 / math.sqrt(all_keys.shape[1])

    def one_head(query_rows):
        scores = (
            lax.dot_general(
                query_rows, all_keys, (((1,), (1,)), ((), ())), preferred_element_type=jnp.float32
            )
            * score_scale
        )
        scores = jnp.where(allowed, scores, -jnp.inf)
        row_max = jnp.max(scores, axis=1, keepdims=True)
        weights = jnp.exp(scores - row_max)
        weights_bf = (weights / jnp.sum(weights, axis=1, keepdims=True)).astype(jnp.bfloat16)
        return jnp.dot(weights_bf, all_values, preferred_element_type=jnp.float32).astype(
            jnp.bfloat16
        )

    outputs = lax.map(one_head, jnp.moveaxis(queries, 1, 0))
    return jnp.moveaxis(outputs, 0, 1).reshape(queries.shape[0], -1)


def scatter_pieces(panels, request_groups):
    local_panels = panels[:, 0]
    held_count = local_panels.shape[0]
    flat_pieces = local_panels.reshape(held_count, request_groups, -1)
    return jnp.moveaxis(flat_pieces, 1, 0)


def on_device(
    hidden,
    base_query_block,
    key_value_block,
    prefix_page_store,
    adapter_down_weight,
    adapter_up_weight,
    request_adapter,
    prefix_page_count,
    page_owner_groups,
    page_pool_row,
):
    request_groups = lax.axis_size("req")
    head_width = key_value_block.shape[1] // 2
    total_row_count = hidden.shape[0]
    page_len = prefix_page_store.shape[1]
    rank_space_rows = adapter_down_weight.shape[2]
    page_count = prefix_page_count[0]
    slot_order = jnp.arange(page_owner_groups.shape[1], dtype=jnp.int32)
    live_slots = slot_order < page_count
    holder_order = jnp.arange(request_groups, dtype=jnp.int32)
    matched = (page_owner_groups[0][None, :] == holder_order[:, None]) & live_slots[None, :]
    wanted = jnp.max(jnp.where(matched, page_pool_row[0][None, :], -1), axis=1)
    asked_for = jnp.stack(
        [wanted, jnp.full((request_groups,), request_adapter[0], jnp.int32)], axis=1
    )
    incoming = lax.all_to_all(asked_for, "req", split_axis=0, concat_axis=0, tiled=True)
    their_pages = jnp.maximum(incoming[:, 0], 0)
    their_adapters = incoming[:, 1]
    spread_down, spread_up = (
        lax.all_to_all(
            scatter_pieces(adapter_down_weight, request_groups),
            "req",
            split_axis=0,
            concat_axis=0,
            tiled=True,
        ),
        lax.all_to_all(
            scatter_pieces(adapter_up_weight, request_groups),
            "req",
            split_axis=0,
            concat_axis=0,
            tiled=True,
        ),
    )
    every_down = spread_down.reshape(-1, spread_down.shape[2])
    every_up = spread_up.reshape(-1, spread_up.shape[2])
    pick_down = jnp.take(every_down, their_adapters, axis=0)
    pick_up = jnp.take(every_up, their_adapters, axis=0)
    down_pieces, up_pieces = (
        lax.all_to_all(pick_down, "req", split_axis=0, concat_axis=0, tiled=True),
        lax.all_to_all(pick_up, "req", split_axis=0, concat_axis=0, tiled=True),
    )
    down_projected_rows = down_pieces.reshape(rank_space_rows, -1)
    up_projected_rows = up_pieces.reshape(rank_space_rows, -1)
    outgoing = jnp.take(prefix_page_store, their_pages, axis=0)
    fetched = lax.all_to_all(outgoing, "req", split_axis=0, concat_axis=0, tiled=True)
    partial_value = lax.dot_general(
        hidden, down_projected_rows, (((1,), (1,)), ((), ())), preferred_element_type=jnp.float32
    )
    rank_reduce = lax.psum(partial_value, "mp").astype(jnp.bfloat16)
    adapter_delta = jnp.dot(rank_reduce, up_projected_rows, preferred_element_type=jnp.float32)
    query_head_count = base_query_block.shape[1] // head_width
    positions = page_len * page_count + jnp.arange(total_row_count, dtype=jnp.int32)
    reduced_sum = (base_query_block.astype(jnp.float32) + adapter_delta).reshape(
        total_row_count, query_head_count, head_width
    )
    queries = rotate(reduced_sum, positions).astype(jnp.bfloat16)
    block_keys = rotate(key_value_block[:, None, :head_width].astype(jnp.float32), positions)[
        :, 0
    ].astype(jnp.bfloat16)
    flat_pages = fetched.reshape(request_groups * page_len, 2 * head_width)
    prefix_mask = jnp.repeat(wanted >= 0, page_len)
    all_keys = jnp.concatenate([flat_pages[:, :head_width], block_keys], axis=0)
    all_values = jnp.concatenate(
        [flat_pages[:, head_width:], key_value_block[:, head_width:]], axis=0
    )
    token_order = jnp.arange(total_row_count, dtype=jnp.int32)
    causal = token_order[:, None] >= token_order[None, :]
    allowed = jnp.concatenate(
        [
            jnp.broadcast_to(prefix_mask[None, :], (total_row_count, request_groups * page_len)),
            causal,
        ],
        axis=1,
    )
    return attend(queries, all_keys, all_values, allowed)


def solution(mesh):
    in_specs = (
        P(("parts", "req"), "mp"),
        P(("parts", "req"), "mp"),
        P(("parts", "req"), None),
        P(("parts", "req"), None, None),
        P("req", "mp", None, None),
        P("req", "mp", None, None),
        P(("parts", "req")),
        P(("parts", "req")),
        P(("parts", "req"), None),
        P(("parts", "req"), None),
    )
    out_specs = P(("parts", "req"), "mp")
    return jax.shard_map(
        on_device, mesh=mesh, in_specs=in_specs, out_specs=out_specs, check_vma=False
    )
```

profile of v0, /device:TPU:0, one launch (start us, length us, event | category | flops | bytes accessed | tf_op | source)
XLA Modules:
  0.0 98.7 jit_solution(5840383050707625583)
XLA Ops:
  1.4 0.6 copy-done.6
  2.2 0.7 copy.33
  2.9 7.3 %all-to-all-start = ((s32[8,1,2]{2,1,0:T(1,128)}), s32[8,1,2]{2,1,0:T(1,128)S(1)}, u32[]{:S(2)}, u32[]{:S(2)}) async-start(s32[8,1,2]{2,1,0:T(1,128)} %copy.33), calls=%async_computation | async-start | bytes 8192 | tf_op jit(solution)/shard_map/all_to_all | solution.py:77
  10.2 2.5 %transpose_reshape_squeeze.8 = bf16[8,1,32768]{2,1,0:T(2,128)(2,1)S(1)} reshape(bf16[1,1,64,4096]{3,2,1,0:T(8,128)(2,1)} %param.16) | data formatting | bytes 1048576 | tf_op jit(solution)/shard_map/transpose;reshape;squeeze | solution.py:48
  12.7 0.6 broadcast.143
  13.3 3.8 %reduce.4 = bf16[8,32768]{1,0:T(8,128)(2,1)S(1)} reduce(bf16[8,1,32768]{2,1,0:T(2,128)(2,1)S(1)} %transpose_reshape_squeeze.8, bf16[]{:T(256)} %broadcast.143), dimensions={1}, to_apply=%transpose_reshape_squeeze.8.reduce_sub_computation | reduce | bytes 1048578 | tf_op jit(solution)/shard_map/transpose;reshape;squeeze | solution.py:48
  17.1 1.2 %reshape.163 = bf16[8,2,16384]{2,1,0:T(2,128)(2,1)} reshape(bf16[8,32768]{1,0:T(8,128)(2,1)S(1)} %reduce.4) | data formatting | bytes 1048576
  18.3 1.0 %reduce.2 = bf16[8,4096]{1,0:T(8,128)(2,1)S(1)} reduce(bf16[8,1,4096]{2,1,0:T(2,128)(2,1)S(1)} %transpose_reshape_squeeze.9, bf16[]{:T(256)} %broadcast.143), dimensions={1}, to_apply=%transpose_reshape_squeeze.9.reduce_sub_computation | reduce | bytes 131074 | tf_op jit(solution)/shard_map/transpose;reshape;squeeze | solution.py:48
  19.3 0.7 reshape.159
  20.3 0.3 multiply_cosine_fusion
  20.7 6.0 %all-to-all-start.3 = ((bf16[8,2,2048]{2,1,0:T(2,128)(2,1)}), bf16[8,2,2048]{2,1,0:T(2,128)(2,1)S(1)}, u32[]{:S(2)}, u32[]{:S(2)}) async-start(bf16[8,2,2048]{2,1,0:T(2,128)(2,1)} %reshape.159), calls=%async_computation.3 | async-start | bytes 131072 | tf_op jit(solution)/shard_map/all_to_all | solution.py:88
  26.8 6.8 %all-to-all-done.3 = bf16[8,2,2048]{2,1,0:T(2,128)(2,1)S(1)} async-done(((bf16[8,2,2048]{2,1,0:T(2,128)(2,1)}), bf16[8,2,2048]{2,1,0:T(2,128)(2,1)S(1)}, u32[]{:S(2)}, u32[]{:S(2)}) %all-to-all-start.3) | async-done | bytes 65568 | tf_op jit(solution)/shard_map/all_to_all | solution.py:88
  33.6 3.5 %all-to-all-start.1 = ((bf16[8,2,16384]{2,1,0:T(2,128)(2,1)}), bf16[8,2,16384]{2,1,0:T(2,128)(2,1)S(1)}, u32[]{:S(2)}, u32[]{:S(2)}) async-start(bf16[8,2,16384]{2,1,0:T(2,128)(2,1)} %reshape.163), calls=%async_computation.1 | async-start | bytes 1048576 | tf_op jit(solution)/shard_map/all_to_all | solution.py:81
  37.1 0.6 gather_fusion.2
  37.8 0.6 gather_fusion.1
  38.5 0.6 reduce.3
  39.2 0.7 reshape.161
  39.8 10.0 %all-to-all-done.1 = bf16[8,2,16384]{2,1,0:T(2,128)(2,1)S(1)} async-done(((bf16[8,2,16384]{2,1,0:T(2,128)(2,1)}), bf16[8,2,16384]{2,1,0:T(2,128)(2,1)S(1)}, u32[]{:S(2)}, u32[]{:S(2)}) %all-to-all-start.1) | async-done | bytes 524320 | tf_op jit(solution)/shard_map/all_to_all | solution.py:81
  49.9 3.6 %all-to-all-start.4 = ((bf16[8,2,2048]{2,1,0:T(2,128)(2,1)}), bf16[8,2,2048]{2,1,0:T(2,128)(2,1)S(1)}, u32[]{:S(2)}, u32[]{:S(2)}) async-start(bf16[8,2,2048]{2,1,0:T(2,128)(2,1)} %reshape.161), calls=%async_computation.4 | async-start | bytes 131072 | tf_op jit(solution)/shard_map/all_to_all | solution.py:102
  53.5 0.7 broadcast_select_fusion
  54.2 0.5 reshape.164
  54.7 0.6 copy.53
  55.3 0.9 gather_fusion
  56.2 4.2 %all-to-all-done.4 = bf16[8,2,2048]{2,1,0:T(2,128)(2,1)S(1)} async-done(((bf16[8,2,2048]{2,1,0:T(2,128)(2,1)}), bf16[8,2,2048]{2,1,0:T(2,128)(2,1)S(1)}, u32[]{:S(2)}, u32[]{:S(2)}) %all-to-all-start.4) | async-done | bytes 65568 | tf_op jit(solution)/shard_map/all_to_all | solution.py:102
  60.4 3.4 %all-to-all-start.5 = ((bf16[8,32,256]{2,1,0:T(8,128)(2,1)}), bf16[8,32,256]{2,1,0:T(8,128)(2,1)S(1)}, u32[]{:S(2)}, u32[]{:S(2)}) async-start(bf16[8,32,256]{2,1,0:T(8,128)(2,1)} %broadcast_select_fusion), calls=%async_computation.5 | async-start | bytes 262144 | tf_op jit(solution)/shard_map/all_to_all | solution.py:107
  63.9 1.0 %reduce.5 = bf16[8,32768]{1,0:T(8,128)(2,1)S(1)} reduce(bf16[8,1,32768]{2,0,1:T(8,128)(2,1)S(1)} %bitcast_select_fusion, bf16[]{:T(256)} %broadcast.143), dimensions={1}, to_apply=%copy.36.reduce_sub_computation | reduce | bytes 1048578 | tf_op jit(solution)/shard_map/jit(_take)/select_n | solution.py:98
  64.9 1.2 %reshape.165 = bf16[8,2,16384]{2,1,0:T(2,128)(2,1)} reshape(bf16[8,32768]{1,0:T(8,128)(2,1)S(1)} %reduce.5) | data formatting | bytes 1048576
  66.0 5.0 %all-to-all-done.5 = bf16[8,32,256]{2,1,0:T(8,128)(2,1)S(1)} async-done(((bf16[8,32,256]{2,1,0:T(8,128)(2,1)}), bf16[8,32,256]{2,1,0:T(8,128)(2,1)S(1)}, u32[]{:S(2)}, u32[]{:S(2)}) %all-to-all-start.5) | async-done | bytes 131104 | tf_op jit(solution)/shard_map/all_to_all | solution.py:107
  71.0 3.7 %all-to-all-start.2 = ((bf16[8,2,16384]{2,1,0:T(2,128)(2,1)}), bf16[8,2,16384]{2,1,0:T(2,128)(2,1)S(1)}, u32[]{:S(2)}, u32[]{:S(2)}) async-start(bf16[8,2,16384]{2,1,0:T(2,128)(2,1)} %reshape.165), calls=%async_computation.2 | async-start | bytes 1048576 | tf_op jit(solution)/shard_map/all_to_all | solution.py:101
  75.0 0.4 reduce.1
  75.5 10.5 %all-to-all-done.2 = bf16[8,2,16384]{2,1,0:T(2,128)(2,1)S(1)} async-done(((bf16[8,2,16384]{2,1,0:T(2,128)(2,1)}), bf16[8,2,16384]{2,1,0:T(2,128)(2,1)S(1)}, u32[]{:S(2)}, u32[]{:S(2)}) %all-to-all-start.2) | async-done | bytes 524320 | tf_op jit(solution)/shard_map/all_to_all | solution.py:101
  85.9 0.5 reshape.166
  86.5 3.2 %reduce = bf16[8,32768]{1,0:T(8,128)(2,1)S(1)} reduce(bf16[8,1,32768]{2,1,0:T(2,128)(2,1)S(1)} %reshape.166, bf16[]{:T(256)} %constant.83), dimensions={1}, to_apply=%all_to_all.29.reduce_sub_computation | reduce | bytes 1048578 | tf_op jit(solution)/shard_map/all_to_all | solution.py:101
  89.6 0.2 reshape.126
  89.9 0.5 convolution_bitcast_fusion
  90.4 3.4 %psum.7 = bf16[128,64]{0,1:T(8,128)(2,1)S(1)} all-reduce(f32[128,64]{0,1:T(8,128)S(1)} %convolution_bitcast_fusion), channel_id=1, replica_groups=mesh['parts'=2,'req'=8,'mp'=2] {'mp'}, use_global_device_ids=true, to_apply=%region_1.2 | all-reduce | flops 8192 | bytes 49152 | tf_op jit(solution)/shard_map/psum | solution.py:111
  93.8 0.2 fusion.9
  94.4 0.7 copy-done.2
  95.1 3.0 %while.10 = (s32[]{:T(128)}, bf16[4,128,128]{2,1,0:T(8,128)(2,1)S(1)}, bf16[4,128,128]{2,1,0:T(8,128)(2,1)S(1)}, bf16[384,128]{1,0:T(8,128)(2,1)S(1)}, pred[128,...) while((s32[]{:T(128)}, bf16[4,128,128]{2,1,0:T(8,128)(2,1)S(1)}, ...), condition=%wide.region_5.6_spmd, body=%wide.region_2.5_spmd.sunk | while | flops 25575168 | bytes 903765 | solution.py:40
  95.1 0.3 fusion.37
  95.6 0.3 fusion.39
  95.9 0.3 fusion.37
  96.3 0.3 fusion.39
  96.6 0.3 fusion.37
  97.1 0.3 fusion.39
  97.3 0.3 fusion.37
  97.8 0.3 fusion.39
  98.1 0.7 copy_bitcast_fusion.2
  (51 shorter events, 2.5 us)
Async XLA Ops:
  0.0 89.9 %copy-start = (bf16[128,4096]{1,0:T(8,128)(2,1)S(1)}, bf16[128,4096]{1,0:T(8,128)(2,1)}, u32[]{:S(2)}) copy-start(bf16[128,4096]{1,0:T(8,128)(2,1)} %param.12) | copy-start | bytes 3145732
  1.4 0.7 copy-start.6
  1.4 0.7 copy-start.7
  2.9 17.8 %all-to-all-start = ((s32[8,1,2]{2,1,0:T(1,128)}), s32[8,1,2]{2,1,0:T(1,128)S(1)}, u32[]{:S(2)}, u32[]{:S(2)}) async-start(s32[8,1,2]{2,1,0:T(1,128)} %copy.33), calls=%async_computation | async-start | bytes 8192 | tf_op jit(solution)/shard_map/all_to_all | solution.py:77
  17.1 1.2 %copy-start.4 = (bf16[1,1,64,512]{3,2,1,0:T(8,128)(2,1)S(1)}, bf16[1,1,64,512]{3,2,1,0:T(8,128)(2,1)}, u32[]{:S(2)}) copy-start(bf16[1,1,64,512]{3,2,1,0:T(8,128)(2,1)} %param.17) | copy-start | bytes 196612
  19.3 0.8 copy-start.1
  20.7 12.9 %all-to-all-start.3 = ((bf16[8,2,2048]{2,1,0:T(2,128)(2,1)}), bf16[8,2,2048]{2,1,0:T(2,128)(2,1)S(1)}, u32[]{:S(2)}, u32[]{:S(2)}) async-start(bf16[8,2,2048]{2,1,0:T(2,128)(2,1)} %reshape.159), calls=%async_computation.3 | async-start | bytes 131072 | tf_op jit(solution)/shard_map/all_to_all | solution.py:88
  26.8 10.3 %copy-start.5 = (bf16[16,32,256]{2,1,0:T(8,128)(2,1)S(1)}, bf16[16,32,256]{2,1,0:T(8,128)(2,1)}, u32[]{:S(2)}) copy-start(bf16[16,32,256]{2,1,0:T(8,128)(2,1)} %param.15) | copy-start | bytes 786436
  33.6 16.3 %all-to-all-start.1 = ((bf16[8,2,16384]{2,1,0:T(2,128)(2,1)}), bf16[8,2,16384]{2,1,0:T(2,128)(2,1)S(1)}, u32[]{:S(2)}, u32[]{:S(2)}) async-start(bf16[8,2,16384]{2,1,0:T(2,128)(2,1)} %reshape.163), calls=%async_computation.1 | async-start | bytes 1048576 | tf_op jit(solution)/shard_map/all_to_all | solution.py:81
  49.9 10.5 %all-to-all-start.4 = ((bf16[8,2,2048]{2,1,0:T(2,128)(2,1)}), bf16[8,2,2048]{2,1,0:T(2,128)(2,1)S(1)}, u32[]{:S(2)}, u32[]{:S(2)}) async-start(bf16[8,2,2048]{2,1,0:T(2,128)(2,1)} %reshape.161), calls=%async_computation.4 | async-start | bytes 131072 | tf_op jit(solution)/shard_map/all_to_all | solution.py:102
  60.4 10.7 %all-to-all-start.5 = ((bf16[8,32,256]{2,1,0:T(8,128)(2,1)}), bf16[8,32,256]{2,1,0:T(8,128)(2,1)S(1)}, u32[]{:S(2)}, u32[]{:S(2)}) async-start(bf16[8,32,256]{2,1,0:T(8,128)(2,1)} %broadcast_select_fusion), calls=%async_computation.5 | async-start | bytes 262144 | tf_op jit(solution)/shard_map/all_to_all | solution.py:107
  71.0 14.9 %all-to-all-start.2 = ((bf16[8,2,16384]{2,1,0:T(2,128)(2,1)}), bf16[8,2,16384]{2,1,0:T(2,128)(2,1)S(1)}, u32[]{:S(2)}, u32[]{:S(2)}) async-start(bf16[8,2,16384]{2,1,0:T(2,128)(2,1)} %reshape.165), calls=%async_computation.2 | async-start | bytes 1048576 | tf_op jit(solution)/shard_map/all_to_all | solution.py:101
  89.9 3.9 %copy-start.3 = (bf16[128,512]{1,0:T(8,128)(2,1)S(1)}, bf16[128,512]{1,0:T(8,128)(2,1)}, u32[]{:S(2)}) copy-start(bf16[128,512]{1,0:T(8,128)(2,1)} %param.13) | copy-start | bytes 393220
  94.2 0.9 copy-start.2
where the time goes:
time: 99.5 us; the launch traced here: 98.7 us
  waiting for transfers between devices  36.4 us (37%)
  starting transfers between devices  27.4 us (28%)
  local copies, waits for them, and re-layouts  14.2 us (14%)
  other arithmetic  12.7 us (13%)
  blocking collectives  3.41 us (3%)
  matrix products  2.79 us (3%)
  between operations  1.8 us (2%)
    all_to_all x1, waiting for transfers between devices, on_device(): lax.all_to_all(pick_down, 'req', split_axis=0, concat_axis=0, tiled=True)  10.5 us
    all_to_all x1, waiting for transfers between devices, on_device(): lax.all_to_all(scatter_pieces(adapter_down_weight, request_groups), 'req'...  10 us
    all_to_all x1, starting transfers between devices, on_device(): lax.all_to_all(asked_for, 'req', split_axis=0, concat_axis=0, tiled=True)  7.25 us
    unnamed x26, local copies, waits for them, and re-layouts  7.1 us
    all_to_all x1, waiting for transfers between devices, on_device(): lax.all_to_all(scatter_pieces(adapter_up_weight, request_groups), 'req',...  6.78 us
    all_to_all x1, starting transfers between devices, on_device(): lax.all_to_all(scatter_pieces(adapter_up_weight, request_groups), 'req',...  6.01 us
    all_to_all x1, waiting for transfers between devices, on_device(): lax.all_to_all(outgoing, 'req', split_axis=0, concat_axis=0, tiled=True)  4.98 us
    another operation x2, other arithmetic, scatter_pieces(): return jnp.moveaxis(flat_pieces, 1, 0)  4.79 us
  transfers between devices with their start and end apart: 6, of which 5 were waited for; matrix products, arithmetic and copies ran while one was open for 19% of the time, Pallas kernels for 0%

commit v1 on v0

v1 whole, which is shorter than its diff:
```python
import math

import jax
import jax.numpy as jnp
from jax import lax
from jax.sharding import PartitionSpec as P

ROPE_BASE = 500000.0
LANES = 128
TILE_ROWS = 16


def rotate(vectors, positions):
    head_width = vectors.shape[-1]
    half_dim = head_width // 2
    frequency = ROPE_BASE ** (-2.0 * jnp.arange(half_dim, dtype=jnp.float32) / head_width)
    angles = positions.astype(jnp.float32)[:, None] * frequency[None, :]
    cosine = jnp.concatenate([jnp.cos(angles), jnp.cos(angles)], axis=1)[:, None, :]
    sine_part = jnp.concatenate([jnp.sin(angles), jnp.sin(angles)], axis=1)[:, None, :]
    turned = jnp.concatenate([-vectors[..., half_dim:], vectors[..., :half_dim]], axis=-1)
    return vectors * cosine + turned * sine_part


def tiled_ok(shape, groups):
    rows, cols = shape
    if rows % TILE_ROWS or cols % LANES:
        return False
    return ((rows // TILE_ROWS) * (cols // LANES)) % groups == 0


def to_pieces(matrix, groups):
    rows, cols = matrix.shape
    if tiled_ok(matrix.shape, groups):
        tiles = matrix.reshape(rows // TILE_ROWS, TILE_ROWS, cols // LANES, LANES)
        tiles = jnp.transpose(tiles, (0, 2, 1, 3))
        return tiles.reshape(groups, -1, LANES)
    flat = matrix.reshape(groups, -1)
    extra = (-flat.shape[1]) % LANES
    if extra:
        flat = jnp.pad(flat, ((0, 0), (0, extra)))
    return flat.reshape(groups, -1, LANES)


def from_pieces(pieces, shape):
    rows, cols = shape
    groups = pieces.shape[0]
    if tiled_ok(shape, groups):
        tiles = pieces.reshape(rows // TILE_ROWS, cols // LANES, TILE_ROWS, LANES)
        tiles = jnp.transpose(tiles, (0, 2, 1, 3))
        return tiles.reshape(rows, cols)
    flat = pieces.reshape(groups, -1)[:, : rows * cols // groups]
    return flat.reshape(rows, cols)


def piece_rows(shape, groups):
    rows, cols = shape
    if tiled_ok(shape, groups):
        return rows * cols // groups // LANES
    return -(-(rows * cols // groups) // LANES)


def attend(queries, all_keys, all_values, allowed):
    token_count, head_count, head_width = queries.shape
    score_scale = 1.0 / math.sqrt(head_width)
    rows = queries.reshape(token_count * head_count, head_width)
    scores = (
        lax.dot_general(
            rows, all_keys, (((1,), (1,)), ((), ())), preferred_element_type=jnp.float32
        )
        * score_scale
    )
    scores = scores.reshape(token_count, head_count, -1)
    scores = jnp.where(allowed[:, None, :], scores, -jnp.inf)
    row_max = jnp.max(scores, axis=2, keepdims=True)
    weights = jnp.exp(scores - row_max)
    weights_bf = (weights / jnp.sum(weights, axis=2, keepdims=True)).astype(jnp.bfloat16)
    out = jnp.dot(
        weights_bf.reshape(token_count * head_count, -1),
        all_values,
        preferred_element_type=jnp.float32,
    ).astype(jnp.bfloat16)
    return out.reshape(token_count, head_count * head_width)


def on_device(
    hidden,
    base_query_block,
    key_value_block,
    prefix_page_store,
    adapter_down_weight,
    adapter_up_weight,
    request_adapter,
    prefix_page_count,
    page_owner_groups,
    page_pool_row,
):
    groups = lax.axis_size("req")
    head_width = key_value_block.shape[1] // 2
    total_row_count = hidden.shape[0]
    page_len = prefix_page_store.shape[1]
    held = adapter_down_weight.shape[0]
    down_shape = adapter_down_weight.shape[2:]
    up_shape = adapter_up_weight.shape[2:]
    down_rows = piece_rows(down_shape, groups)
    up_rows = piece_rows(up_shape, groups)

    page_count = prefix_page_count[0]
    slot_order = jnp.arange(page_owner_groups.shape[1], dtype=jnp.int32)
    live_slots = slot_order < page_count
    holder_order = jnp.arange(groups, dtype=jnp.int32)
    matched = (page_owner_groups[0][None, :] == holder_order[:, None]) & live_slots[None, :]
    wanted = jnp.max(jnp.where(matched, page_pool_row[0][None, :], -1), axis=1)

    asks = jnp.zeros((groups, 1, LANES), jnp.float32)
    asks = asks.at[:, 0, 0].set(jnp.maximum(wanted, 0).astype(jnp.float32))
    asks = asks.at[:, 0, 1].set(request_adapter[0].astype(jnp.float32))
    parts_out = []
    for a in range(held):
        parts_out.append(to_pieces(adapter_down_weight[a, 0], groups))
        parts_out.append(to_pieces(adapter_up_weight[a, 0], groups))
    parts_out.append(asks.astype(jnp.bfloat16))
    stage_one = jnp.concatenate(parts_out, axis=1)
    stage_one = lax.all_to_all(stage_one, "req", split_axis=0, concat_axis=0, tiled=True)

    share_rows = down_rows + up_rows
    shares = stage_one[:, : held * share_rows].reshape(groups * held, share_rows, LANES)
    their_asks = stage_one[:, held * share_rows, :2].astype(jnp.int32)
    their_pages = their_asks[:, 0]
    their_adapters = their_asks[:, 1]

    picked = jnp.take(shares, their_adapters, axis=0)
    pages = jnp.take(prefix_page_store, their_pages, axis=0)
    page_pieces = jax.vmap(lambda page: to_pieces(page, 1)[0])(pages)
    stage_two = jnp.concatenate([picked, page_pieces], axis=1)
    stage_two = lax.all_to_all(stage_two, "req", split_axis=0, concat_axis=0, tiled=True)

    down_projected_rows = from_pieces(stage_two[:, :down_rows], down_shape)
    up_projected_rows = from_pieces(stage_two[:, down_rows:share_rows], up_shape)
    fetched = jax.vmap(lambda piece: from_pieces(piece[None], (page_len, 2 * head_width)))(
        stage_two[:, share_rows:]
    )

    partial_value = lax.dot_general(
        hidden, down_projected_rows, (((1,), (1,)), ((), ())), preferred_element_type=jnp.float32
    )
    rank_reduce = lax.psum(partial_value, "mp").astype(jnp.bfloat16)
    adapter_delta = jnp.dot(rank_reduce, up_projected_rows, preferred_element_type=jnp.float32)
    query_head_count = base_query_block.shape[1] // head_width
    positions = page_len * page_count + jnp.arange(total_row_count, dtype=jnp.int32)
    reduced_sum = (base_query_block.astype(jnp.float32) + adapter_delta).reshape(
        total_row_count, query_head_count, head_width
    )
    queries = rotate(reduced_sum, positions).astype(jnp.bfloat16)
    block_keys = rotate(key_value_block[:, None, :head_width].astype(jnp.float32), positions)[
        :, 0
    ].astype(jnp.bfloat16)
    flat_pages = fetched.reshape(groups * page_len, 2 * head_width)
    prefix_mask = jnp.repeat(wanted >= 0, page_len)
    all_keys = jnp.concatenate([flat_pages[:, :head_width], block_keys], axis=0)
    all_values = jnp.concatenate(
        [flat_pages[:, head_width:], key_value_block[:, head_width:]], axis=0
    )
    token_order = jnp.arange(total_row_count, dtype=jnp.int32)
    causal = token_order[:, None] >= token_order[None, :]
    allowed = jnp.concatenate(
        [
            jnp.broadcast_to(prefix_mask[None, :], (total_row_count, groups * page_len)),
            causal,
        ],
        axis=1,
    )
    return attend(queries, all_keys, all_values, allowed)


def solution(mesh):
    in_specs = (
        P(("parts", "req"), "mp"),
        P(("parts", "req"), "mp"),
        P(("parts", "req"), None),
        P(("parts", "req"), None, None),
        P("req", "mp", None, None),
        P("req", "mp", None, None),
        P(("parts", "req")),
        P(("parts", "req")),
        P(("parts", "req"), None),
        P(("parts", "req"), None),
    )
    out_specs = P(("parts", "req"), "mp")
    return jax.shard_map(
        on_device, mesh=mesh, in_specs=in_specs, out_specs=out_specs, check_vma=False
    )
```

time: 99.5 us -> 64.9 us (0.65)
  starting transfers between devices: 27.4 us -> 11 us
  other arithmetic: 12.7 us -> 3.15 us
  local copies, waits for them, and re-layouts: 14.2 us -> 9.87 us
  waiting for transfers between devices: 36.4 us -> 33.7 us
  matrix products: 2.79 us -> 1.43 us
    all_to_all x6 -> x2, starting transfers between devices: 27.4 us -> 11 us  [the longest x1 7.25 us: on_device(): lax.all_to_all(stage_one, 'req', split_axis=0, concat_axis=0, tiled=True)]
    another operation x2 -> x0, other arithmetic: 4.79 us -> none  [scatter_pieces(): return jnp.moveaxis(flat_pieces, 1, 0)]
    unnamed x26 -> x14, local copies, waits for them, and re-layouts: 7.1 us -> 2.72 us
    all_to_all x2 -> x0, other arithmetic: 3.54 us -> none  [the longest x1 3.17 us: on_device(): lax.all_to_all(pick_down, 'req', split_axis=0, concat_axis=0, tiled=True)]
    all_to_all x6 -> x2, waiting for transfers between devices: 36.4 us -> 33.7 us  [the longest x1 17.7 us: on_device(): lax.all_to_all(stage_two, 'req', split_axis=0, concat_axis=0, tiled=True)]
    another operation x3 -> x4, local copies, waits for them, and re-layouts: 3.11 us -> 0.68 us  [scatter_pieces(): return jnp.moveaxis(flat_pieces, 1, 0)]
    select_n x5 -> x2, other arithmetic: 2.57 us -> 0.17 us  [on_device(): picked = jnp.take(shares, their_adapters, axis=0)]
    dot_general x8 -> x2, matrix products: 2.1 us -> 0.74 us  [the longest x1 0.42 us: attend(): lax.dot_general(rows, all_keys, (((1,), (1,)), ((), ())), preferred_eleme...]
  transfers between devices with their start and end apart: 6 -> 2, of which waited for: 5 -> 2; matrix products, arithmetic and copies ran while one was open for 19% -> 2% of each run, Pallas kernels for 0% -> 0%
where the time goes in v1:
time: 64.9 us; the launch traced here: 64.4 us
  waiting for transfers between devices  33.7 us (52%)
  starting transfers between devices  11 us (17%)
  local copies, waits for them, and re-layouts  9.87 us (15%)
  blocking collectives  3.41 us (5%)
  other arithmetic  3.15 us (5%)
  between operations  1.79 us (3%)
  matrix products  1.43 us (2%)
    all_to_all x1, waiting for transfers between devices, on_device(): lax.all_to_all(stage_two, 'req', split_axis=0, concat_axis=0, tiled=True)  17.7 us
    all_to_all x1, waiting for transfers between devices, on_device(): lax.all_to_all(stage_one, 'req', split_axis=0, concat_axis=0, tiled=True)  16 us
    all_to_all x1, starting transfers between devices, on_device(): lax.all_to_all(stage_one, 'req', split_axis=0, concat_axis=0, tiled=True)  7.25 us
    all_to_all x1, starting transfers between devices, on_device(): lax.all_to_all(stage_two, 'req', split_axis=0, concat_axis=0, tiled=True)  3.77 us
    psum x1, blocking collectives, on_device(): rank_reduce = lax.psum(partial_value, 'mp').astype(jnp.bfloat16)  3.41 us
    unnamed x14, local copies, waits for them, and re-layouts  2.72 us
    scatter x1, local copies, waits for them, and re-layouts, on_device(): asks = asks.at[:, 0, 1].set(request_adapter[0].astype(jnp.float32))  1.33 us
  transfers between devices with their start and end apart: 2, of which 2 were waited for; matrix products, arithmetic and copies ran while one was open for 2% of the time, Pallas kernels for 0%

profile of v1, /device:TPU:0, one launch (start us, length us, event | category | flops | bytes accessed | tf_op | source)
XLA Modules:
  0.0 64.4 jit_solution(6399788822573083362)
XLA Ops:
  0.0 0.0 copy-start
  0.8 0.8 %select_reduce_fusion = s32[8]{0:T(128)S(1)} fusion(s32[8]{0:T(128)} %bitcast.92, s32[8]{0:T(128)} %bitcast.93, pred[8]{0:T(512)(128)(4,1)S(1)} %iota_compare_fusion.2), kind=kLoop, calls=%fused_computation.48 | loop fusion | flops 248 | bytes 104 | tf_op jit(solution)/shard_map/reduce_max | solution.py:112
  1.6 0.1 copy.78
  2.3 0.7 %slice.88 = s32[1]{0:T(128)} slice(s32[2]{0:T(128)S(1)} %iota.33), slice={[1:2]} | slice | bytes 8 | tf_op jit(solution)/shard_map/slice.52
  3.0 1.1 %copy.90 = bf16[8,8,32,128]{3,2,1,0:T(8,128)(2,1)S(1)} copy(bf16[8,8,32,128]{3,1,2,0:T(8,128)(2,1)} %bitcast.84) | data formatting | bytes 1048576
  4.1 0.0 copy-start.4
  4.2 0.2 copy.76
  4.4 0.6 copy-done.4
  5.0 1.3 %scatter.9 = bf16[8,1,128]{2,1,0:T(2,128)(2,1)S(1)} dynamic-update-slice(bf16[8,1,128]{2,1,0:T(2,128)(2,1)S(1)} %scatter.6, bf16[8,1,1]{2,1,0:T(2,128)(2,1)S(1)} %broadcast.132, s32[]{:T(128)} %constant.94.clone.1, s32[]{:T(128)} %constant.94.clone.1, s32[]{:T(128)} %bitcast.9) | dynamic-update-slice | bytes 36 | tf_op jit(solution)/shard_map/scatter | solution.py:116
  6.4 0.9 %pad_maximum_fusion.1 = bf16[8,289,128]{2,1,0:T(8,128)(2,1)} fusion(bf16[8,1,128]{2,1,0:T(2,128)(2,1)S(1)} %scatter.9, bf16[8,32,128]{2,1,0:T(8,128)(2,1)S(1)} %bitcast.88, bf16[8,256,128]{2,1,0:T(8,128)(2,1)S(1)} %bitcast.76), kind=kLoop, calls=%fused_computation.12 | loop fusion | flops 1775616 | bytes 1183744 | tf_op jit(solution)/shard_map/concatenate | solution.py:122
  7.2 7.3 %all-to-all-start = ((bf16[8,289,128]{2,1,0:T(8,128)(2,1)}), bf16[8,289,128]{2,1,0:T(8,128)(2,1)S(1)}, u32[]{:S(2)}, u32[]{:S(2)}) async-start(bf16[8,289,128]{2,1,0:T(8,128)(2,1)} %pad_maximum_fusion.1), calls=%async_computation | async-start | bytes 1212416 | tf_op jit(solution)/shard_map/all_to_all | solution.py:123
  14.5 0.1 broadcast_in_dim.82
  14.6 0.1 reshape.188
  14.7 16.0 %all-to-all-done = bf16[8,289,128]{2,1,0:T(8,128)(2,1)S(1)} async-done(((bf16[8,289,128]{2,1,0:T(8,128)(2,1)}), bf16[8,289,128]{2,1,0:T(8,128)(2,1)S(1)}, u32[]{:S(2)}, u32[]{:S(2)}) %all-to-all-start) | async-done | bytes 591904 | tf_op jit(solution)/shard_map/all_to_all | solution.py:123
  30.7 0.1 copy.88
  30.9 0.0 copy-start.3
  30.9 0.4 copy.89
  31.3 0.5 copy-done.3
  31.8 0.6 gather_fusion.1
  32.4 0.2 fusion.7
  32.6 0.2 copy.82
  32.8 0.7 %gather_fusion = bf16[8,288,128]{1,2,0:T(8,128)(2,1)S(1)} fusion(bf16[8,288,128]{1,2,0:T(8,128)(2,1)S(1)} %copy.89, s32[1024]{0:T(1024)S(1)} %get-tuple-element.49), kind=kCustom, calls=%fused_computation | custom fusion | bytes 1179680 | tf_op jit(solution)/shard_map/jit(_take)/gather | solution.py:131
  33.6 0.2 broadcast_select_fusion
  33.7 0.2 pad_maximum_fusion
  33.9 1.1 %copy.83 = bf16[8,352,128]{2,1,0:T(8,128)(2,1)} copy(bf16[8,352,128]{1,2,0:T(8,128)(2,1)S(1)} %pad_maximum_fusion) | data formatting | bytes 1441792 | tf_op jit(solution)/shard_map/concatenate | solution.py:134
  35.0 3.8 %all-to-all-start.1 = ((bf16[8,352,128]{2,1,0:T(8,128)(2,1)}), bf16[8,352,128]{2,1,0:T(8,128)(2,1)S(1)}, u32[]{:S(2)}, u32[]{:S(2)}) async-start(bf16[8,352,128]{2,1,0:T(8,128)(2,1)} %copy.83), calls=%async_computation.1 | async-start | bytes 1441792 | tf_op jit(solution)/shard_map/all_to_all | solution.py:135
  38.8 0.2 broadcast_in_dim.85
  39.0 0.2 broadcast_in_dim.86
  39.2 0.3 copy.87
  39.5 0.0 copy-done.1
  39.5 0.3 multiply_cosine_fusion
  39.8 0.1 fusion.18
  39.9 0.1 fusion.15
  40.1 17.7 %all-to-all-done.1 = bf16[8,352,128]{2,1,0:T(8,128)(2,1)S(1)} async-done(((bf16[8,352,128]{2,1,0:T(8,128)(2,1)}), bf16[8,352,128]{2,1,0:T(8,128)(2,1)S(1)}, u32[]{:S(2)}, u32[]{:S(2)}) %all-to-all-start.1) | async-done | bytes 720928 | tf_op jit(solution)/shard_map/all_to_all | solution.py:135
  57.8 0.1 copy.84
  57.9 0.0 copy-start.2
  57.9 0.0 copy-done
  57.9 0.5 convolution_bitcast_fusion
  58.4 3.4 %psum.7 = bf16[128,64]{0,1:T(8,128)(2,1)S(1)} all-reduce(f32[128,64]{0,1:T(8,128)S(1)} %convolution_bitcast_fusion), channel_id=1, replica_groups=mesh['parts'=2,'req'=8,'mp'=2] {'mp'}, use_global_device_ids=true, to_apply=%region_1.2 | all-reduce | flops 8192 | bytes 49152 | tf_op jit(solution)/shard_map/psum | solution.py:146
  61.9 0.0 copy-done.2
  61.9 0.2 convolution_add_fusion
  62.1 0.1 reshape.168
  62.2 0.2 slice_negate_fusion
  62.5 0.1 copy.86
  62.7 0.4 fusion.28
  63.2 0.2 fusion.1
  63.3 0.3 convolution_convert_fusion
  63.6 0.7 %reshape.170 = bf16[128,512]{1,0:T(8,128)(2,1)} reshape(bf16[512,128]{1,0:T(8,128)(2,1)S(1)} %convolution_convert_fusion) | data formatting | bytes 262144 | tf_op jit(solution)/shard_map/reshape | solution.py:82
  (33 shorter events, 0.5 us)
Async XLA Ops:
  0.0 57.9 %copy-start = (bf16[128,4096]{1,0:T(8,128)(2,1)S(1)}, bf16[128,4096]{1,0:T(8,128)(2,1)}, u32[]{:S(2)}) copy-start(bf16[128,4096]{1,0:T(8,128)(2,1)} %param.14) | copy-start | bytes 3145732
  4.1 0.8 %copy-start.4 = (bf16[1,1,64,512]{3,2,1,0:T(8,128)(2,1)S(1)}, bf16[1,1,64,512]{3,2,1,0:T(8,128)(2,1)}, u32[]{:S(2)}) copy-start(bf16[1,1,64,512]{3,2,1,0:T(8,128)(2,1)} %param.19) | copy-start | bytes 196612
  7.2 23.5 %all-to-all-start = ((bf16[8,289,128]{2,1,0:T(8,128)(2,1)}), bf16[8,289,128]{2,1,0:T(8,128)(2,1)S(1)}, u32[]{:S(2)}, u32[]{:S(2)}) async-start(bf16[8,289,128]{2,1,0:T(8,128)(2,1)} %pad_maximum_fusion.1), calls=%async_computation | async-start | bytes 1212416 | tf_op jit(solution)/shard_map/all_to_all | solution.py:123
  30.9 1.0 %copy-start.3 = (bf16[16,32,256]{2,1,0:T(8,128)(2,1)S(1)}, bf16[16,32,256]{2,1,0:T(8,128)(2,1)}, u32[]{:S(2)}) copy-start(bf16[16,32,256]{2,1,0:T(8,128)(2,1)} %param.17) | copy-start | bytes 786436
  35.0 4.5 %copy-start.1 = (bf16[128,256]{1,0:T(8,128)(2,1)S(1)}, bf16[128,256]{1,0:T(8,128)(2,1)}, u32[]{:S(2)}) copy-start(bf16[128,256]{1,0:T(8,128)(2,1)} %param.16) | copy-start | bytes 196612
  35.0 22.7 %all-to-all-start.1 = ((bf16[8,352,128]{2,1,0:T(8,128)(2,1)}), bf16[8,352,128]{2,1,0:T(8,128)(2,1)S(1)}, u32[]{:S(2)}, u32[]{:S(2)}) async-start(bf16[8,352,128]{2,1,0:T(8,128)(2,1)} %copy.83), calls=%async_computation.1 | async-start | bytes 1441792 | tf_op jit(solution)/shard_map/all_to_all | solution.py:135
  57.9 4.0 %copy-start.2 = (bf16[128,512]{1,0:T(8,128)(2,1)S(1)}, bf16[128,512]{1,0:T(8,128)(2,1)}, u32[]{:S(2)}) copy-start(bf16[128,512]{1,0:T(8,128)(2,1)} %param.15) | copy-start | bytes 393220

commit v2 on v1

--- a/solution.py
+++ b/solution.py
@@ -7,7 +7,7 @@
 
 ROPE_BASE = 500000.0
 LANES = 128
-TILE_ROWS = 16
+TILE_ROWS = 8
 
 
 def rotate(vectors, positions):
@@ -111,39 +111,78 @@
     matched = (page_owner_groups[0][None, :] == holder_order[:, None]) & live_slots[None, :]
     wanted = jnp.max(jnp.where(matched, page_pool_row[0][None, :], -1), axis=1)
 
-    asks = jnp.zeros((groups, 1, LANES), jnp.float32)
-    asks = asks.at[:, 0, 0].set(jnp.maximum(wanted, 0).astype(jnp.float32))
-    asks = asks.at[:, 0, 1].set(request_adapter[0].astype(jnp.float32))
-    parts_out = []
-    for a in range(held):
-        parts_out.append(to_pieces(adapter_down_weight[a, 0], groups))
-        parts_out.append(to_pieces(adapter_up_weight[a, 0], groups))
-    parts_out.append(asks.astype(jnp.bfloat16))
-    stage_one = jnp.concatenate(parts_out, axis=1)
-    stage_one = lax.all_to_all(stage_one, "req", split_axis=0, concat_axis=0, tiled=True)
-
-    share_rows = down_rows + up_rows
-    shares = stage_one[:, : held * share_rows].reshape(groups * held, share_rows, LANES)
-    their_asks = stage_one[:, held * share_rows, :2].astype(jnp.int32)
-    their_pages = their_asks[:, 0]
-    their_adapters = their_asks[:, 1]
-
-    picked = jnp.take(shares, their_adapters, axis=0)
-    pages = jnp.take(prefix_page_store, their_pages, axis=0)
-    page_pieces = jax.vmap(lambda page: to_pieces(page, 1)[0])(pages)
-    stage_two = jnp.concatenate([picked, page_pieces], axis=1)
-    stage_two = lax.all_to_all(stage_two, "req", split_axis=0, concat_axis=0, tiled=True)
-
-    down_projected_rows = from_pieces(stage_two[:, :down_rows], down_shape)
-    up_projected_rows = from_pieces(stage_two[:, down_rows:share_rows], up_shape)
-    fetched = jax.vmap(lambda piece: from_pieces(piece[None], (page_len, 2 * head_width)))(
-        stage_two[:, share_rows:]
-    )
+    page_shape = prefix_page_store.shape[1:]
+    row_block = down_shape[0] // groups if down_shape[0] % groups == 0 else 0
+    fast = (
+        row_block > 0
+        and row_block % TILE_ROWS == 0
+        and up_shape[0] == down_shape[0]
+        and (page_shape[0] * page_shape[1]) % (row_block * LANES) == 0
+    )
+    lane = lax.broadcasted_iota(jnp.int32, (groups, LANES), 1)
+    asks = jnp.where(
+        lane == 0,
+        jnp.maximum(wanted, 0)[:, None],
+        jnp.where(lane == 1, request_adapter[0], 0),
+    ).astype(jnp.bfloat16)
+
+    if fast:
+        down_cols = down_shape[1]
+        share_cols = down_cols + up_shape[1]
+        ask_rows = jnp.broadcast_to(asks[:, None, :], (groups, row_block, LANES))
+        parts_out = []
+        for a in range(held):
+            parts_out.append(adapter_down_weight[a, 0].reshape(groups, row_block, -1))
+            parts_out.append(adapter_up_weight[a, 0].reshape(groups, row_block, -1))
+        parts_out.append(ask_rows)
+        stage_one = jnp.concatenate(parts_out, axis=2)
+        stage_one = lax.all_to_all(stage_one, "req", split_axis=0, concat_axis=0, tiled=True)
+        shares = stage_one[:, :, : held * share_cols]
+        shares = shares.reshape(groups, row_block, held, share_cols)
+        shares = jnp.moveaxis(shares, 2, 1).reshape(groups * held, row_block, share_cols)
+        their_asks = stage_one[:, 0, held * share_cols : held * share_cols + 2].astype(jnp.int32)
+        their_pages = their_asks[:, 0]
+        their_adapters = their_asks[:, 1]
+        picked = jnp.take(shares, their_adapters, axis=0)
+        pages = jnp.take(prefix_page_store, their_pages, axis=0).reshape(groups, row_block, -1)
+        stage_two = jnp.concatenate([picked, pages], axis=2)
+        stage_two = lax.all_to_all(stage_two, "req", split_axis=0, concat_axis=0, tiled=True)
+        down_projected_rows = stage_two[:, :, :down_cols].reshape(down_shape)
+        up_projected_rows = stage_two[:, :, down_cols:share_cols].reshape(up_shape)
+        fetched = stage_two[:, :, share_cols:].reshape((groups,) + page_shape)
+    else:
+        parts_out = []
+        for a in range(held):
+            parts_out.append(to_pieces(adapter_down_weight[a, 0], groups))
+            parts_out.append(to_pieces(adapter_up_weight[a, 0], groups))
+        parts_out.append(asks[:, None, :])
+        stage_one = jnp.concatenate(parts_out, axis=1)
+        stage_one = lax.all_to_all(stage_one, "req", split_axis=0, concat_axis=0, tiled=True)
+        share_rows = down_rows + up_rows
+        shares = stage_one[:, : held * share_rows].reshape(groups * held, share_rows, LANES)
+        their_asks = stage_one[:, held * share_rows, :2].astype(jnp.int32)
+        their_pages = their_asks[:, 0]
+        their_adapters = their_asks[:, 1]
+        picked = jnp.take(shares, their_adapters, axis=0)
+        pages = jnp.take(prefix_page_store, their_pages, axis=0)
+        page_pieces = jax.vmap(lambda page: to_pieces(page, 1)[0])(pages)
+        stage_two = jnp.concatenate([picked, page_pieces], axis=1)
+        stage_two = lax.all_to_all(stage_two, "req", split_axis=0, concat_axis=0, tiled=True)
+        down_projected_rows = from_pieces(stage_two[:, :down_rows], down_shape)
+        up_projected_rows = from_pieces(stage_two[:, down_rows:share_rows], up_shape)
+        fetched = jax.vmap(lambda piece: from_pieces(piece[None], page_shape))(
+            stage_two[:, share_rows:]
+        )
 
     partial_value = lax.dot_general(
         hidden, down_projected_rows, (((1,), (1,)), ((), ())), preferred_element_type=jnp.float32
     )
-    rank_reduce = lax.psum(partial_value, "mp").astype(jnp.bfloat16)
+    mp_count = lax.axis_size("mp")
+    if mp_count == 2:
+        partner = lax.ppermute(partial_value, "mp", [(0, 1), (1, 0)])
+        rank_reduce = (partial_value + partner).astype(jnp.bfloat16)
+    else:
+        rank_reduce = lax.psum(partial_value, "mp").astype(jnp.bfloat16)
     adapter_delta = jnp.dot(rank_reduce, up_projected_rows, preferred_element_type=jnp.float32)
     query_head_count = base_query_block.shape[1] // head_width
     positions = page_len * page_count + jnp.arange(total_row_count, dtype=jnp.int32)

time: 64.9 us -> 57.5 us (0.89)
  local copies, waits for them, and re-layouts: 9.87 us -> 3.25 us
  blocking collectives: 3.41 us -> 0 us
  other arithmetic: 3.15 us -> 4.95 us
  waiting for transfers between devices: 33.7 us -> 34.8 us
    psum x1 -> x0, blocking collectives: 3.41 us -> none  [on_device(): rank_reduce = lax.psum(partial_value, 'mp').astype(jnp.bfloat16)]
    unnamed x14 -> x9, local copies, waits for them, and re-layouts: 2.72 us -> 0.12 us
    concatenate x2, other arithmetic: 1.04 us -> 2.9 us  [the longest x1 1.99 us: on_device(): stage_one = jnp.concatenate(parts_out, axis=2)]
    scatter x2 -> x0, local copies, waits for them, and re-layouts: 1.34 us -> none  [the longest x1 1.33 us: on_device(): asks = asks.at[:, 0, 1].set(request_adapter[0].astype(jnp.float32))]
    concatenate x1 -> x0, local copies, waits for them, and re-layouts: 1.15 us -> none  [on_device(): stage_two = jnp.concatenate([picked, page_pieces], axis=1)]
    ppermute x0 -> x1, waiting for transfers between devices: none -> 1.06 us  [on_device(): partner = lax.ppermute(partial_value, 'mp', [(0, 1), (1, 0)])]
  transfers between devices with their start and end apart: 2 -> 3, of which waited for: 2 -> 3; matrix products, arithmetic and copies ran while one was open for 2% -> 3% of each run, Pallas kernels for 0% -> 0%
where the time goes in v2:
time: 57.5 us; the launch traced here: 57.1 us
  waiting for transfers between devices  34.8 us (61%)
  starting transfers between devices  11.1 us (19%)
  other arithmetic  4.95 us (9%)
  local copies, waits for them, and re-layouts  3.25 us (6%)
  between operations  1.66 us (3%)
  matrix products  1.42 us (2%)
    all_to_all x1, waiting for transfers between devices, on_device(): lax.all_to_all(stage_two, 'req', split_axis=0, concat_axis=0, tiled=True)  17.7 us
    all_to_all x1, waiting for transfers between devices, on_device(): lax.all_to_all(stage_one, 'req', split_axis=0, concat_axis=0, tiled=True)  16 us
    all_to_all x1, starting transfers between devices, on_device(): lax.all_to_all(stage_one, 'req', split_axis=0, concat_axis=0, tiled=True)  7.25 us
    all_to_all x1, starting transfers between devices, on_device(): lax.all_to_all(stage_two, 'req', split_axis=0, concat_axis=0, tiled=True)  3.77 us
    concatenate x1, other arithmetic, on_device(): stage_one = jnp.concatenate(parts_out, axis=2)  1.99 us
  transfers between devices with their start and end apart: 3, of which 3 were waited for; matrix products, arithmetic and copies ran while one was open for 3% of the time, Pallas kernels for 0%

profile of v2, /device:TPU:0, one launch (start us, length us, event | category | flops | bytes accessed | tf_op | source)
XLA Modules:
  0.0 57.1 jit_solution(6103449483649919813)
XLA Ops:
  0.0 0.0 copy-start
  1.4 0.8 %select_reduce_fusion = s32[8]{0:T(128)S(1)} fusion(s32[8]{0:T(128)} %bitcast.45, s32[8]{0:T(128)} %bitcast.46, pred[8]{0:T(512)(128)(4,1)S(1)} %iota_compare_fusion.3), kind=kLoop, calls=%fused_computation.44 | loop fusion | flops 248 | bytes 104 | tf_op jit(solution)/shard_map/reduce_max | solution.py:112
  2.2 0.1 select_convert_fusion
  2.3 0.0 copy-start.3
  2.3 2.0 %pad_maximum_fusion.1 = bf16[8,8,4736]{2,1,0:T(8,128)(2,1)} fusion(bf16[8,8,128]{2,1,0:T(8,128)(2,1)S(1)} %broadcast_in_dim.105, bf16[8,8,512]{2,1,0:T(8,128)(2,1)} %bitcast.44, bf16[8,8,4096]{2,1,0:T(8,128)(2,1)} %bitcast.43), kind=kLoop, calls=%fused_computation.11 | loop fusion | flops 1818624 | bytes 1212416 | tf_op jit(solution)/shard_map/concatenate | solution.py:138
  4.3 7.3 %all-to-all-start = ((bf16[8,8,4736]{2,1,0:T(8,128)(2,1)}), bf16[8,8,4736]{2,1,0:T(8,128)(2,1)S(1)}, u32[]{:S(2)}, u32[]{:S(2)}) async-start(bf16[8,8,4736]{2,1,0:T(8,128)(2,1)} %pad_maximum_fusion.1), calls=%async_computation | async-start | bytes 1212416 | tf_op jit(solution)/shard_map/all_to_all | solution.py:139
  11.6 0.1 broadcast_in_dim.98
  11.6 0.1 reshape.130
  11.7 16.0 %all-to-all-done = bf16[8,8,4736]{2,1,0:T(8,128)(2,1)S(1)} async-done(((bf16[8,8,4736]{2,1,0:T(8,128)(2,1)}), bf16[8,8,4736]{2,1,0:T(8,128)(2,1)S(1)}, u32[]{:S(2)}, u32[]{:S(2)}) %all-to-all-start) | async-done | bytes 606240 | tf_op jit(solution)/shard_map/all_to_all | solution.py:139
  27.8 0.1 copy.26
  27.9 0.0 copy-done.3
  28.0 0.6 gather_fusion.1
  28.5 0.1 gather.12
  28.7 0.6 %gather_fusion = bf16[8,8,4608]{2,1,0:T(8,128)(2,1)S(1)} fusion(bf16[8,8,4608]{2,1,0:T(8,128)(2,1)S(1)} %slice.65, s32[1024]{0:T(1024)S(1)} %get-tuple-element.25), kind=kCustom, calls=%fused_computation | custom fusion | bytes 1179680 | tf_op jit(solution)/shard_map/jit(_take)/gather | solution.py:146
  29.3 0.1 broadcast_select_fusion
  29.4 0.1 broadcast_select_fusion.1
  29.5 0.9 %pad_maximum_fusion = bf16[8,8,5632]{2,1,0:T(8,128)(2,1)} fusion(bf16[8,8,1024]{2,1,0:T(8,128)(2,1)S(1)} %broadcast_select_fusion.1, bf16[8,8,4608]{2,1,0:T(8,128)(2,1)S(1)} %broadcast_select_fusion), kind=kLoop, calls=%fused_computation.9 | loop fusion | flops 1441792 | bytes 1441792 | tf_op jit(solution)/shard_map/concatenate | solution.py:148
  30.4 0.0 copy-start.1
  30.4 3.8 %all-to-all-start.1 = ((bf16[8,8,5632]{2,1,0:T(8,128)(2,1)}), bf16[8,8,5632]{2,1,0:T(8,128)(2,1)S(1)}, u32[]{:S(2)}, u32[]{:S(2)}) async-start(bf16[8,8,5632]{2,1,0:T(8,128)(2,1)} %pad_maximum_fusion), calls=%async_computation.1 | async-start | bytes 1441792 | tf_op jit(solution)/shard_map/all_to_all | solution.py:149
  34.2 0.2 broadcast_in_dim.101
  34.4 0.2 broadcast_in_dim.102
  34.5 0.3 copy.25
  34.8 0.0 copy-done.1
  34.9 0.3 multiply_cosine_fusion
  35.2 0.1 fusion.13
  35.3 0.1 fusion.12
  35.4 0.0 copy-start.2
  35.4 17.7 %all-to-all-done.1 = bf16[8,8,5632]{2,1,0:T(8,128)(2,1)S(1)} async-done(((bf16[8,8,5632]{2,1,0:T(8,128)(2,1)}), bf16[8,8,5632]{2,1,0:T(8,128)(2,1)S(1)}, u32[]{:S(2)}, u32[]{:S(2)}) %all-to-all-start.1) | async-done | bytes 720928 | tf_op jit(solution)/shard_map/all_to_all | solution.py:149
  53.1 0.0 copy-done
  53.1 0.5 convolution_bitcast_fusion
  53.6 0.1 collective-permute-start
  53.7 0.1 reshape_reshape.3
  53.8 1.1 %collective-permute-done = f32[128,64]{0,1:T(8,128)S(1)} collective-permute-done((f32[128,64]{0,1:T(8,128)S(1)}, f32[128,64]{0,1:T(8,128)S(1)}, u32[]{:S(2)}, u32[]{:S(2)}) %collective-permute-start) | collective-permute-done | bytes 32800 | tf_op jit(solution)/shard_map/ppermute | solution.py:182
  54.8 0.0 copy-done.2
  54.8 0.2 convolution_add_fusion
  55.1 0.1 reshape.111
  55.2 0.2 slice_negate_fusion
  55.5 0.4 fusion.22
  55.9 0.2 fusion.1
  56.1 0.3 convolution_convert_fusion
  56.4 0.7 %reshape.112 = bf16[128,512]{1,0:T(8,128)(2,1)} reshape(bf16[512,128]{1,0:T(8,128)(2,1)S(1)} %convolution_convert_fusion) | data formatting | bytes 262144 | tf_op jit(solution)/shard_map/reshape | solution.py:82
  (23 shorter events, 0.3 us)
Async XLA Ops:
  0.0 53.1 %copy-start = (bf16[128,4096]{1,0:T(8,128)(2,1)S(1)}, bf16[128,4096]{1,0:T(8,128)(2,1)}, u32[]{:S(2)}) copy-start(bf16[128,4096]{1,0:T(8,128)(2,1)} %param.10) | copy-start | bytes 3145732
  2.3 25.6 %copy-start.3 = (bf16[16,32,256]{2,1,0:T(8,128)(2,1)S(1)}, bf16[16,32,256]{2,1,0:T(8,128)(2,1)}, u32[]{:S(2)}) copy-start(bf16[16,32,256]{2,1,0:T(8,128)(2,1)} %param.13) | copy-start | bytes 786436
  4.3 23.5 %all-to-all-start = ((bf16[8,8,4736]{2,1,0:T(8,128)(2,1)}), bf16[8,8,4736]{2,1,0:T(8,128)(2,1)S(1)}, u32[]{:S(2)}, u32[]{:S(2)}) async-start(bf16[8,8,4736]{2,1,0:T(8,128)(2,1)} %pad_maximum_fusion.1), calls=%async_computation | async-start | bytes 1212416 | tf_op jit(solution)/shard_map/all_to_all | solution.py:139
  30.4 4.5 %copy-start.1 = (bf16[128,256]{1,0:T(8,128)(2,1)S(1)}, bf16[128,256]{1,0:T(8,128)(2,1)}, u32[]{:S(2)}) copy-start(bf16[128,256]{1,0:T(8,128)(2,1)} %param.12) | copy-start | bytes 196612
  30.4 22.7 %all-to-all-start.1 = ((bf16[8,8,5632]{2,1,0:T(8,128)(2,1)}), bf16[8,8,5632]{2,1,0:T(8,128)(2,1)S(1)}, u32[]{:S(2)}, u32[]{:S(2)}) async-start(bf16[8,8,5632]{2,1,0:T(8,128)(2,1)} %pad_maximum_fusion), calls=%async_computation.1 | async-start | bytes 1441792 | tf_op jit(solution)/shard_map/all_to_all | solution.py:149
  35.4 19.4 %copy-start.2 = (bf16[128,512]{1,0:T(8,128)(2,1)S(1)}, bf16[128,512]{1,0:T(8,128)(2,1)}, u32[]{:S(2)}) copy-start(bf16[128,512]{1,0:T(8,128)(2,1)} %param.11) | copy-start | bytes 393220
  53.6 1.3 %collective-permute-start = (f32[128,64]{0,1:T(8,128)S(1)}, f32[128,64]{0,1:T(8,128)S(1)}, u32[]{:S(2)}, u32[]{:S(2)}) collective-permute-start(f32[128,64]{0,1:T(8,128)S(1)} %convolution_bitcast_fusion), channel_id=1, source_target_pairs={{0,1},{1,0},{2,3},{3,2},{4,5},{5,4},{6,7},{7,6},{8,9},{9,8},{10,11... | collective-permute-start | bytes 98312 | tf_op jit(solution)/shard_map/ppermute | solution.py:182

commit v3 on v2

--- a/solution.py
+++ b/solution.py
@@ -3,6 +3,8 @@
 import jax
 import jax.numpy as jnp
 from jax import lax
+from jax.experimental import pallas as pl
+from jax.experimental.pallas import tpu as pltpu
 from jax.sharding import PartitionSpec as P
 
 ROPE_BASE = 500000.0
@@ -19,6 +21,36 @@
     sine_part = jnp.concatenate([jnp.sin(angles), jnp.sin(angles)], axis=1)[:, None, :]
     turned = jnp.concatenate([-vectors[..., half_dim:], vectors[..., :half_dim]], axis=-1)
     return vectors * cosine + turned * sine_part
+
+
+def pack_kernel(*refs):
+    *sources, out_ref, sems = refs
+    copies = []
+    start = 0
+    for index, source in enumerate(sources):
+        width = source.shape[2]
+        copies.append(
+            pltpu.make_async_copy(
+                source, out_ref.at[:, :, pl.ds(start, width)], sems.at[index]
+            )
+        )
+        start += width
+    for copy in copies:
+        copy.start()
+    for copy in copies:
+        copy.wait()
+
+
+def pack_lanes(sources):
+    lead = sources[0].shape[:2]
+    width = sum(source.shape[2] for source in sources)
+    return pl.pallas_call(
+        pack_kernel,
+        out_shape=jax.ShapeDtypeStruct(lead + (width,), sources[0].dtype),
+        in_specs=[pl.BlockSpec(memory_space=pl.ANY)] * len(sources),
+        out_specs=pl.BlockSpec(memory_space=pl.ANY),
+        scratch_shapes=[pltpu.SemaphoreType.DMA((len(sources),))],
+    )(*sources)
 
 
 def tiled_ok(shape, groups):
@@ -135,7 +167,7 @@
             parts_out.append(adapter_down_weight[a, 0].reshape(groups, row_block, -1))
             parts_out.append(adapter_up_weight[a, 0].reshape(groups, row_block, -1))
         parts_out.append(ask_rows)
-        stage_one = jnp.concatenate(parts_out, axis=2)
+        stage_one = pack_lanes(parts_out)
         stage_one = lax.all_to_all(stage_one, "req", split_axis=0, concat_axis=0, tiled=True)
         shares = stage_one[:, :, : held * share_cols]
         shares = shares.reshape(groups, row_block, held, share_cols)
@@ -143,8 +175,8 @@
         their_asks = stage_one[:, 0, held * share_cols : held * share_cols + 2].astype(jnp.int32)
         their_pages = their_asks[:, 0]
         their_adapters = their_asks[:, 1]
-        picked = jnp.take(shares, their_adapters, axis=0)
-        pages = jnp.take(prefix_page_store, their_pages, axis=0).reshape(groups, row_block, -1)
+        picked = jnp.take(shares, their_adapters, axis=0, mode="clip")
+        pages = jnp.take(prefix_page_store, their_pages, axis=0, mode="clip").reshape(groups, row_block, -1)
         stage_two = jnp.concatenate([picked, pages], axis=2)
         stage_two = lax.all_to_all(stage_two, "req", split_axis=0, concat_axis=0, tiled=True)
         down_projected_rows = stage_two[:, :, :down_cols].reshape(down_shape)
@@ -163,8 +195,8 @@
         their_asks = stage_one[:, held * share_rows, :2].astype(jnp.int32)
         their_pages = their_asks[:, 0]
         their_adapters = their_asks[:, 1]
-        picked = jnp.take(shares, their_adapters, axis=0)
-        pages = jnp.take(prefix_page_store, their_pages, axis=0)
+        picked = jnp.take(shares, their_adapters, axis=0, mode="clip")
+        pages = jnp.take(prefix_page_store, their_pages, axis=0, mode="clip")
         page_pieces = jax.vmap(lambda page: to_pieces(page, 1)[0])(pages)
         stage_two = jnp.concatenate([picked, page_pieces], axis=1)
         stage_two = lax.all_to_all(stage_two, "req", split_axis=0, concat_axis=0, tiled=True)

time: 57.5 us -> 75.3 us (1.31)
  Pallas kernels: 0 us -> 19.5 us
  other arithmetic: 4.95 us -> 2.75 us
    pallas_call x0 -> x1, Pallas kernels: none -> 19.5 us  [pack_lanes(): pl.pallas_call(pack_kernel, out_shape=jax.ShapeDtypeStruct(lead + (width,...]
    concatenate x1 -> x0, other arithmetic: 1.99 us -> none  [on_device(): stage_one = jnp.concatenate(parts_out, axis=2)]
  transfers between devices with their start and end apart: 3 -> 3, of which waited for: 3 -> 3; matrix products, arithmetic and copies ran while one was open for 3% -> 2% of each run, Pallas kernels for 0% -> 0%
where the time goes in v3:
time: 75.3 us; the launch traced here: 75 us
  waiting for transfers between devices  34.8 us (46%)
  Pallas kernels  19.5 us (26%)
  starting transfers between devices  11.1 us (15%)
  local copies, waits for them, and re-layouts  3.84 us (5%)
  other arithmetic  2.75 us (4%)
  between operations  1.63 us (2%)
  matrix products  1.42 us (2%)
    pallas_call x1, Pallas kernels, pack_lanes(): pl.pallas_call(pack_kernel, out_shape=jax.ShapeDtypeStruct(lead + (width,...  19.5 us
    all_to_all x1, waiting for transfers between devices, on_device(): lax.all_to_all(stage_two, 'req', split_axis=0, concat_axis=0, tiled=True)  17.7 us
    all_to_all x1, waiting for transfers between devices, on_device(): lax.all_to_all(stage_one, 'req', split_axis=0, concat_axis=0, tiled=True)  16 us
    all_to_all x1, starting transfers between devices, on_device(): lax.all_to_all(stage_one, 'req', split_axis=0, concat_axis=0, tiled=True)  7.26 us
    all_to_all x1, starting transfers between devices, on_device(): lax.all_to_all(stage_two, 'req', split_axis=0, concat_axis=0, tiled=True)  3.77 us
  transfers between devices with their start and end apart: 3, of which 3 were waited for; matrix products, arithmetic and copies ran while one was open for 2% of the time, Pallas kernels for 0%

profile of v3, /device:TPU:0, one launch (start us, length us, event | category | flops | bytes accessed | tf_op | source)
XLA Modules:
  0.0 75.0 jit_solution(3778216328950301713)
XLA Ops:
  0.0 0.0 copy-start
  1.4 0.8 %select_reduce_fusion = s32[8]{0:T(128)S(1)} fusion(s32[8]{0:T(128)} %bitcast.40, s32[8]{0:T(128)} %bitcast.41, pred[8]{0:T(512)(128)(4,1)S(1)} %iota_compare_fusion.3), kind=kLoop, calls=%fused_computation.42 | loop fusion | flops 248 | bytes 104 | tf_op jit(solution)/shard_map/reduce_max | solution.py:144
  2.2 0.1 select_convert_fusion
  2.3 0.6 broadcast_in_dim.89.refs_2_
  2.9 0.0 copy-start.3
  2.9 19.5 %shard_map.100 = bf16[8,8,4736]{2,1,0:T(8,128)(2,1)} custom-call(bf16[8,8,4096]{2,1,0:T(8,128)(2,1)} %bitcast.37, bf16[8,8,512]{2,1,0:T(8,128)(2,1)} %bitcast.38, bf16[8,8,128]{2,1,0:T(8,128)(2,1)} %broadcast_in_dim.89.refs_2_), custom_call_target="tpu_custom_call" | custom-call | tf_op jit(solution)/shard_map/pallas_call | solution.py:47
  22.4 7.3 %all-to-all-start = ((bf16[8,8,4736]{2,1,0:T(8,128)(2,1)}), bf16[8,8,4736]{2,1,0:T(8,128)(2,1)S(1)}, u32[]{:S(2)}, u32[]{:S(2)}) async-start(bf16[8,8,4736]{2,1,0:T(8,128)(2,1)} %shard_map.100), calls=%async_computation | async-start | bytes 1212416 | tf_op jit(solution)/shard_map/all_to_all | solution.py:171
  29.7 0.1 broadcast_in_dim.82
  29.8 0.1 reshape.124
  29.9 16.0 %all-to-all-done = bf16[8,8,4736]{2,1,0:T(8,128)(2,1)S(1)} async-done(((bf16[8,8,4736]{2,1,0:T(8,128)(2,1)}), bf16[8,8,4736]{2,1,0:T(8,128)(2,1)S(1)}, u32[]{:S(2)}, u32[]{:S(2)}) %all-to-all-start) | async-done | bytes 606240 | tf_op jit(solution)/shard_map/all_to_all | solution.py:171
  45.9 0.1 copy.16
  46.0 0.0 copy-done.3
  46.0 0.6 gather_fusion.1
  46.6 0.1 reshape.101
  46.7 0.6 gather_fusion
  47.3 0.9 %pad_maximum_fusion = bf16[8,8,5632]{2,1,0:T(8,128)(2,1)} fusion(bf16[8,8,1024]{2,1,0:T(8,128)(2,1)S(1)} %reshape.101, bf16[8,8,4608]{2,1,0:T(8,128)(2,1)S(1)} %gather_fusion), kind=kLoop, calls=%fused_computation.9 | loop fusion | flops 1441792 | bytes 1441792 | tf_op jit(solution)/shard_map/concatenate | solution.py:180
  48.2 0.0 copy-start.1
  48.3 3.8 %all-to-all-start.1 = ((bf16[8,8,5632]{2,1,0:T(8,128)(2,1)}), bf16[8,8,5632]{2,1,0:T(8,128)(2,1)S(1)}, u32[]{:S(2)}, u32[]{:S(2)}) async-start(bf16[8,8,5632]{2,1,0:T(8,128)(2,1)} %pad_maximum_fusion), calls=%async_computation.1 | async-start | bytes 1441792 | tf_op jit(solution)/shard_map/all_to_all | solution.py:181
  52.0 0.2 broadcast_in_dim.85
  52.2 0.2 broadcast_in_dim.86
  52.4 0.3 copy.17
  52.7 0.0 copy-done.1
  52.7 0.3 multiply_cosine_fusion
  53.0 0.1 fusion.13
  53.1 0.1 fusion.12
  53.3 0.0 copy-start.2
  53.3 17.7 %all-to-all-done.1 = bf16[8,8,5632]{2,1,0:T(8,128)(2,1)S(1)} async-done(((bf16[8,8,5632]{2,1,0:T(8,128)(2,1)}), bf16[8,8,5632]{2,1,0:T(8,128)(2,1)S(1)}, u32[]{:S(2)}, u32[]{:S(2)}) %all-to-all-start.1) | async-done | bytes 720928 | tf_op jit(solution)/shard_map/all_to_all | solution.py:181
  71.0 0.0 copy-done
  71.0 0.5 convolution_bitcast_fusion
  71.4 0.1 collective-permute-start
  71.5 0.1 reshape_reshape.3
  71.7 1.1 %collective-permute-done = f32[128,64]{0,1:T(8,128)S(1)} collective-permute-done((f32[128,64]{0,1:T(8,128)S(1)}, f32[128,64]{0,1:T(8,128)S(1)}, u32[]{:S(2)}, u32[]{:S(2)}) %collective-permute-start) | collective-permute-done | bytes 32800 | tf_op jit(solution)/shard_map/ppermute | solution.py:214
  72.7 0.0 copy-done.2
  72.7 0.2 convolution_add_fusion
  72.9 0.1 reshape.105
  73.1 0.2 slice_negate_fusion
  73.4 0.4 fusion.20
  73.8 0.2 fusion.1
  73.9 0.3 convolution_convert_fusion
  74.3 0.7 reshape.106
  (20 shorter events, 0.3 us)
Async XLA Ops:
  0.0 71.0 %copy-start = (bf16[128,4096]{1,0:T(8,128)(2,1)S(1)}, bf16[128,4096]{1,0:T(8,128)(2,1)}, u32[]{:S(2)}) copy-start(bf16[128,4096]{1,0:T(8,128)(2,1)} %param.10) | copy-start | bytes 3145732
  2.9 43.1 %copy-start.3 = (bf16[16,32,256]{2,1,0:T(8,128)(2,1)S(1)}, bf16[16,32,256]{2,1,0:T(8,128)(2,1)}, u32[]{:S(2)}) copy-start(bf16[16,32,256]{2,1,0:T(8,128)(2,1)} %param.13) | copy-start | bytes 786436
  22.4 23.5 %all-to-all-start = ((bf16[8,8,4736]{2,1,0:T(8,128)(2,1)}), bf16[8,8,4736]{2,1,0:T(8,128)(2,1)S(1)}, u32[]{:S(2)}, u32[]{:S(2)}) async-start(bf16[8,8,4736]{2,1,0:T(8,128)(2,1)} %shard_map.100), calls=%async_computation | async-start | bytes 1212416 | tf_op jit(solution)/shard_map/all_to_all | solution.py:171
  48.2 4.5 %copy-start.1 = (bf16[128,256]{1,0:T(8,128)(2,1)S(1)}, bf16[128,256]{1,0:T(8,128)(2,1)}, u32[]{:S(2)}) copy-start(bf16[128,256]{1,0:T(8,128)(2,1)} %param.12) | copy-start | bytes 196612
  48.3 22.7 %all-to-all-start.1 = ((bf16[8,8,5632]{2,1,0:T(8,128)(2,1)}), bf16[8,8,5632]{2,1,0:T(8,128)(2,1)S(1)}, u32[]{:S(2)}, u32[]{:S(2)}) async-start(bf16[8,8,5632]{2,1,0:T(8,128)(2,1)} %pad_maximum_fusion), calls=%async_computation.1 | async-start | bytes 1441792 | tf_op jit(solution)/shard_map/all_to_all | solution.py:181
  53.3 19.4 %copy-start.2 = (bf16[128,512]{1,0:T(8,128)(2,1)S(1)}, bf16[128,512]{1,0:T(8,128)(2,1)}, u32[]{:S(2)}) copy-start(bf16[128,512]{1,0:T(8,128)(2,1)} %param.11) | copy-start | bytes 393220
  71.4 1.3 %collective-permute-start = (f32[128,64]{0,1:T(8,128)S(1)}, f32[128,64]{0,1:T(8,128)S(1)}, u32[]{:S(2)}, u32[]{:S(2)}) collective-permute-start(f32[128,64]{0,1:T(8,128)S(1)} %convolution_bitcast_fusion), channel_id=1, source_target_pairs={{0,1},{1,0},{2,3},{3,2},{4,5},{5,4},{6,7},{7,6},{8,9},{9,8},{10,11... | collective-permute-start | bytes 98312 | tf_op jit(solution)/shard_map/ppermute | solution.py:214

commit v4 on v2

--- a/solution.py
+++ b/solution.py
@@ -119,6 +119,12 @@
         and up_shape[0] == down_shape[0]
         and (page_shape[0] * page_shape[1]) % (row_block * LANES) == 0
     )
+    split_pages = (
+        fast
+        and lax.axis_size("mp") == 2
+        and page_shape[0] % 2 == 0
+        and (page_shape[0] // 2 * page_shape[1]) % (row_block * LANES) == 0
+    )
     lane = lax.broadcasted_iota(jnp.int32, (groups, LANES), 1)
     asks = jnp.where(
         lane == 0,
@@ -143,13 +149,21 @@
         their_asks = stage_one[:, 0, held * share_cols : held * share_cols + 2].astype(jnp.int32)
         their_pages = their_asks[:, 0]
         their_adapters = their_asks[:, 1]
-        picked = jnp.take(shares, their_adapters, axis=0)
-        pages = jnp.take(prefix_page_store, their_pages, axis=0).reshape(groups, row_block, -1)
-        stage_two = jnp.concatenate([picked, pages], axis=2)
+        picked = jnp.take(shares, their_adapters, axis=0, mode="clip")
+        pages = jnp.take(prefix_page_store, their_pages, axis=0, mode="clip")
+        if split_pages:
+            half_rows = page_shape[0] // 2
+            pages = lax.dynamic_slice_in_dim(pages, lax.axis_index("mp") * half_rows, half_rows, 1)
+        stage_two = jnp.concatenate([picked, pages.reshape(groups, row_block, -1)], axis=2)
         stage_two = lax.all_to_all(stage_two, "req", split_axis=0, concat_axis=0, tiled=True)
         down_projected_rows = stage_two[:, :, :down_cols].reshape(down_shape)
         up_projected_rows = stage_two[:, :, down_cols:share_cols].reshape(up_shape)
-        fetched = stage_two[:, :, share_cols:].reshape((groups,) + page_shape)
+        if split_pages:
+            mine = stage_two[:, :, share_cols:].reshape(groups, half_rows, page_shape[1])
+            other = lax.ppermute(mine, "mp", [(0, 1), (1, 0)])
+            fetched = jnp.concatenate([mine, other], axis=1)
+        else:
+            fetched = stage_two[:, :, share_cols:].reshape((groups,) + page_shape)
     else:
         parts_out = []
         for a in range(held):
@@ -163,8 +177,8 @@
         their_asks = stage_one[:, held * share_rows, :2].astype(jnp.int32)
         their_pages = their_asks[:, 0]
         their_adapters = their_asks[:, 1]
-        picked = jnp.take(shares, their_adapters, axis=0)
-        pages = jnp.take(prefix_page_store, their_pages, axis=0)
+        picked = jnp.take(shares, their_adapters, axis=0, mode="clip")
+        pages = jnp.take(prefix_page_store, their_pages, axis=0, mode="clip")
         page_pieces = jax.vmap(lambda page: to_pieces(page, 1)[0])(pages)
         stage_two = jnp.concatenate([picked, page_pieces], axis=1)
         stage_two = lax.all_to_all(stage_two, "req", split_axis=0, concat_axis=0, tiled=True)

time: 57.5 us -> 56.1 us (0.976)
  waiting for transfers between devices: 34.8 us -> 33.3 us
    ppermute x1, waiting for transfers between devices: 1.06 us -> 0.01 us  [on_device(): partner = lax.ppermute(partial_value, 'mp', [(0, 1), (1, 0)])]
    all_to_all x1, waiting for transfers between devices: 17.7 us -> 16.7 us  [on_device(): lax.all_to_all(stage_two, 'req', split_axis=0, concat_axis=0, tiled=True)]
    gather x3 -> x2, local copies, waits for them, and re-layouts: 1.23 us -> 1.14 us  [the longest x1 0.59 us: on_device(): picked = jnp.take(shares, their_adapters, axis=0, mode='clip')]
  transfers between devices with their start and end apart: 3 -> 4, of which waited for: 3 -> 3; matrix products, arithmetic and copies ran while one was open for 3% -> 3% of each run, Pallas kernels for 0% -> 0%
where the time goes in v4:
time: 56.1 us; the launch traced here: 55.7 us
  waiting for transfers between devices  33.3 us (59%)
  starting transfers between devices  11.5 us (20%)
  other arithmetic  4.72 us (8%)
  local copies, waits for them, and re-layouts  3.14 us (6%)
  between operations  1.64 us (3%)
  matrix products  1.43 us (3%)
    all_to_all x1, waiting for transfers between devices, on_device(): lax.all_to_all(stage_two, 'req', split_axis=0, concat_axis=0, tiled=True)  16.7 us
    all_to_all x1, waiting for transfers between devices, on_device(): lax.all_to_all(stage_one, 'req', split_axis=0, concat_axis=0, tiled=True)  16.2 us
    all_to_all x1, starting transfers between devices, on_device(): lax.all_to_all(stage_one, 'req', split_axis=0, concat_axis=0, tiled=True)  7.25 us
    all_to_all x1, starting transfers between devices, on_device(): lax.all_to_all(stage_two, 'req', split_axis=0, concat_axis=0, tiled=True)  3.64 us
    concatenate x1, other arithmetic, on_device(): stage_one = jnp.concatenate(parts_out, axis=2)  1.99 us
  transfers between devices with their start and end apart: 4, of which 3 were waited for; matrix products, arithmetic and copies ran while one was open for 3% of the time, Pallas kernels for 0%

profile of v4, /device:TPU:0, one launch (start us, length us, event | category | flops | bytes accessed | tf_op | source)
XLA Modules:
  0.0 55.7 jit_solution(5230457845501905238)
XLA Ops:
  0.0 0.0 copy-start
  1.4 0.8 %select_reduce_fusion = s32[8]{0:T(128)S(1)} fusion(s32[8]{0:T(128)} %bitcast.43, s32[8]{0:T(128)} %bitcast.44, pred[8]{0:T(512)(128)(4,1)S(1)} %iota_compare_fusion.3), kind=kLoop, calls=%fused_computation.43 | loop fusion | flops 248 | bytes 104 | tf_op jit(solution)/shard_map/reduce_max | solution.py:112
  2.2 0.1 select_convert_fusion
  2.3 0.0 copy-start.3
  2.3 2.0 %pad_maximum_fusion.1 = bf16[8,8,4736]{2,1,0:T(8,128)(2,1)} fusion(bf16[8,8,128]{2,1,0:T(8,128)(2,1)S(1)} %broadcast_in_dim.89, bf16[8,8,512]{2,1,0:T(8,128)(2,1)} %bitcast.42, bf16[8,8,4096]{2,1,0:T(8,128)(2,1)} %bitcast.40), kind=kLoop, calls=%fused_computation.11 | loop fusion | flops 1818624 | bytes 1212416 | tf_op jit(solution)/shard_map/concatenate | solution.py:144
  4.3 7.3 %all-to-all-start = ((bf16[8,8,4736]{2,1,0:T(8,128)(2,1)}), bf16[8,8,4736]{2,1,0:T(8,128)(2,1)S(1)}, u32[]{:S(2)}, u32[]{:S(2)}) async-start(bf16[8,8,4736]{2,1,0:T(8,128)(2,1)} %pad_maximum_fusion.1), calls=%async_computation | async-start | bytes 1212416 | tf_op jit(solution)/shard_map/all_to_all | solution.py:145
  11.6 16.2 %all-to-all-done = bf16[8,8,4736]{2,1,0:T(8,128)(2,1)S(1)} async-done(((bf16[8,8,4736]{2,1,0:T(8,128)(2,1)}), bf16[8,8,4736]{2,1,0:T(8,128)(2,1)S(1)}, u32[]{:S(2)}, u32[]{:S(2)}) %all-to-all-start) | async-done | bytes 606240 | tf_op jit(solution)/shard_map/all_to_all | solution.py:145
  27.8 0.1 copy.25
  27.9 0.0 copy-done.3
  27.9 0.6 gather_fusion.1
  28.6 0.6 %gather_fusion = bf16[8,8,4608]{2,1,0:T(8,128)(2,1)S(1)} fusion(bf16[8,8,4608]{2,1,0:T(8,128)(2,1)S(1)} %slice.64, s32[1024]{0:T(1024)S(1)} %get-tuple-element.23), kind=kCustom, calls=%fused_computation | custom fusion | bytes 1179680 | tf_op jit(solution)/shard_map/jit(_take)/gather | solution.py:152
  29.2 0.0 copy-start.1
  29.2 0.9 %pad_maximum_fusion = bf16[8,8,5120]{2,1,0:T(8,128)(2,1)} fusion(bf16[8,8,512]{2,1,0:T(8,128)(2,1)S(1)} %reshape.107, bf16[8,8,4608]{2,1,0:T(8,128)(2,1)S(1)} %gather_fusion), kind=kLoop, calls=%fused_computation.10 | loop fusion | flops 1310720 | bytes 1310720 | tf_op jit(solution)/shard_map/concatenate | solution.py:157
  30.1 3.6 %all-to-all-start.1 = ((bf16[8,8,5120]{2,1,0:T(8,128)(2,1)}), bf16[8,8,5120]{2,1,0:T(8,128)(2,1)S(1)}, u32[]{:S(2)}, u32[]{:S(2)}) async-start(bf16[8,8,5120]{2,1,0:T(8,128)(2,1)} %pad_maximum_fusion), calls=%async_computation.1 | async-start | bytes 1310720 | tf_op jit(solution)/shard_map/all_to_all | solution.py:158
  33.7 0.1 broadcast_in_dim.82
  33.8 0.1 reshape.132
  33.9 0.0 copy-done.1
  34.0 0.3 multiply_cosine_fusion
  34.3 0.1 fusion.13
  34.4 0.1 fusion.12
  34.5 16.7 %all-to-all-done.1 = bf16[8,8,5120]{2,1,0:T(8,128)(2,1)S(1)} async-done(((bf16[8,8,5120]{2,1,0:T(8,128)(2,1)}), bf16[8,8,5120]{2,1,0:T(8,128)(2,1)S(1)}, u32[]{:S(2)}, u32[]{:S(2)}) %all-to-all-start.1) | async-done | bytes 655392 | tf_op jit(solution)/shard_map/all_to_all | solution.py:158
  51.2 0.0 copy-done
  51.2 0.5 convolution_bitcast_fusion
  51.7 0.0 copy-start.2
  51.7 0.1 collective-permute-start
  51.8 0.2 broadcast_in_dim.85
  52.0 0.2 broadcast_in_dim.86
  52.2 0.3 copy.24
  52.5 0.6 collective-permute-start.1
  53.1 0.0 collective-permute-done
  53.1 0.0 copy-done.2
  53.1 0.2 convolution_add_fusion
  53.3 0.1 reshape.111
  53.4 0.2 slice_negate_fusion
  53.6 0.3 collective-permute-done.1
  54.1 0.4 fusion.20
  54.5 0.2 fusion.1
  54.7 0.3 convolution_convert_fusion
  55.0 0.7 %reshape.114 = bf16[128,512]{1,0:T(8,128)(2,1)} reshape(bf16[512,128]{1,0:T(8,128)(2,1)S(1)} %convolution_convert_fusion) | data formatting | bytes 262144 | tf_op jit(solution)/shard_map/reshape | solution.py:82
  (26 shorter events, 0.4 us)
Async XLA Ops:
  0.0 51.2 %copy-start = (bf16[128,4096]{1,0:T(8,128)(2,1)S(1)}, bf16[128,4096]{1,0:T(8,128)(2,1)}, u32[]{:S(2)}) copy-start(bf16[128,4096]{1,0:T(8,128)(2,1)} %param.10) | copy-start | bytes 3145732
  2.3 25.6 %copy-start.3 = (bf16[16,32,256]{2,1,0:T(8,128)(2,1)S(1)}, bf16[16,32,256]{2,1,0:T(8,128)(2,1)}, u32[]{:S(2)}) copy-start(bf16[16,32,256]{2,1,0:T(8,128)(2,1)} %param.13) | copy-start | bytes 786436
  4.3 23.5 %all-to-all-start = ((bf16[8,8,4736]{2,1,0:T(8,128)(2,1)}), bf16[8,8,4736]{2,1,0:T(8,128)(2,1)S(1)}, u32[]{:S(2)}, u32[]{:S(2)}) async-start(bf16[8,8,4736]{2,1,0:T(8,128)(2,1)} %pad_maximum_fusion.1), calls=%async_computation | async-start | bytes 1212416 | tf_op jit(solution)/shard_map/all_to_all | solution.py:145
  29.2 4.8 %copy-start.1 = (bf16[128,256]{1,0:T(8,128)(2,1)S(1)}, bf16[128,256]{1,0:T(8,128)(2,1)}, u32[]{:S(2)}) copy-start(bf16[128,256]{1,0:T(8,128)(2,1)} %param.12) | copy-start | bytes 196612
  30.1 21.1 %all-to-all-start.1 = ((bf16[8,8,5120]{2,1,0:T(8,128)(2,1)}), bf16[8,8,5120]{2,1,0:T(8,128)(2,1)S(1)}, u32[]{:S(2)}, u32[]{:S(2)}) async-start(bf16[8,8,5120]{2,1,0:T(8,128)(2,1)} %pad_maximum_fusion), calls=%async_computation.1 | async-start | bytes 1310720 | tf_op jit(solution)/shard_map/all_to_all | solution.py:158
  51.7 1.4 %copy-start.2 = (bf16[128,512]{1,0:T(8,128)(2,1)S(1)}, bf16[128,512]{1,0:T(8,128)(2,1)}, u32[]{:S(2)}) copy-start(bf16[128,512]{1,0:T(8,128)(2,1)} %param.11) | copy-start | bytes 393220
  51.7 1.4 %collective-permute-start = (f32[128,64]{0,1:T(8,128)S(1)}, f32[128,64]{0,1:T(8,128)S(1)}, u32[]{:S(2)}, u32[]{:S(2)}) collective-permute-start(f32[128,64]{0,1:T(8,128)S(1)} %convolution_bitcast_fusion), channel_id=1, source_target_pairs={{0,1},{1,0},{2,3},{3,2},{4,5},{5,4},{6,7},{7,6},{8,9},{9,8},{10,11... | collective-permute-start | bytes 98312 | tf_op jit(solution)/shard_map/ppermute | solution.py:196
  52.5 1.5 %collective-permute-start.1 = (bf16[8,16,256]{2,1,0:T(8,128)(2,1)S(1)}, bf16[8,16,256]{2,1,0:T(8,128)(2,1)S(1)}, u32[]{:S(2)}, u32[]{:S(2)}) collective-permute-start(bf16[8,16,256]{2,1,0:T(8,128)(2,1)S(1)} %reshape.112), channel_id=1, source_target_pairs={{0,1},{1,0},{2,3},{3,2},{4,5},{5,4},{6,7},{7,6},{8,9},{9,8},{10,11... | collective-permute-start | bytes 196616 | tf_op jit(solution)/shard_map/ppermute | solution.py:163

commit v5 on v4

--- a/solution.py
+++ b/solution.py
@@ -62,24 +62,22 @@
 def attend(queries, all_keys, all_values, allowed):
     token_count, head_count, head_width = queries.shape
     score_scale = 1.0 / math.sqrt(head_width)
-    rows = queries.reshape(token_count * head_count, head_width)
+    rows = jnp.transpose(queries, (1, 0, 2)).reshape(head_count * token_count, head_width)
     scores = (
         lax.dot_general(
             rows, all_keys, (((1,), (1,)), ((), ())), preferred_element_type=jnp.float32
         )
         * score_scale
     )
-    scores = scores.reshape(token_count, head_count, -1)
-    scores = jnp.where(allowed[:, None, :], scores, -jnp.inf)
-    row_max = jnp.max(scores, axis=2, keepdims=True)
+    scores = jnp.where(jnp.tile(allowed, (head_count, 1)), scores, -jnp.inf)
+    row_max = jnp.max(scores, axis=1, keepdims=True)
     weights = jnp.exp(scores - row_max)
-    weights_bf = (weights / jnp.sum(weights, axis=2, keepdims=True)).astype(jnp.bfloat16)
-    out = jnp.dot(
-        weights_bf.reshape(token_count * head_count, -1),
-        all_values,
-        preferred_element_type=jnp.float32,
-    ).astype(jnp.bfloat16)
-    return out.reshape(token_count, head_count * head_width)
+    weights_bf = (weights / jnp.sum(weights, axis=1, keepdims=True)).astype(jnp.bfloat16)
+    out = jnp.dot(weights_bf, all_values, preferred_element_type=jnp.float32).astype(
+        jnp.bfloat16
+    )
+    out = lax.optimization_barrier(out).reshape(head_count, token_count, head_width)
+    return jnp.transpose(out, (1, 0, 2)).reshape(token_count, head_count * head_width)
 
 
 def on_device(

time: 56.1 us -> 55.5 us (0.989)
  local copies, waits for them, and re-layouts: 3.14 us -> 2.46 us
    broadcast_in_dim x3 -> x0, local copies, waits for them, and re-layouts: 0.62 us -> none  [attend(): scores = jnp.where(allowed[:, None, :], scores, -jnp.inf)]
  transfers between devices with their start and end apart: 4 -> 4, of which waited for: 3 -> 3; matrix products, arithmetic and copies ran while one was open for 3% -> 2% of each run, Pallas kernels for 0% -> 0%
where the time goes in v5:
time: 55.5 us; the launch traced here: 55.2 us
  waiting for transfers between devices  33.4 us (60%)
  starting transfers between devices  11.5 us (21%)
  other arithmetic  4.89 us (9%)
  local copies, waits for them, and re-layouts  2.46 us (4%)
  between operations  1.63 us (3%)
  matrix products  1.31 us (2%)
    all_to_all x1, waiting for transfers between devices, on_device(): lax.all_to_all(stage_two, 'req', split_axis=0, concat_axis=0, tiled=True)  16.7 us
    all_to_all x1, waiting for transfers between devices, on_device(): lax.all_to_all(stage_one, 'req', split_axis=0, concat_axis=0, tiled=True)  16.2 us
    all_to_all x1, starting transfers between devices, on_device(): lax.all_to_all(stage_one, 'req', split_axis=0, concat_axis=0, tiled=True)  7.25 us
    all_to_all x1, starting transfers between devices, on_device(): lax.all_to_all(stage_two, 'req', split_axis=0, concat_axis=0, tiled=True)  3.64 us
    concatenate x1, other arithmetic, on_device(): stage_one = jnp.concatenate(parts_out, axis=2)  1.99 us
  transfers between devices with their start and end apart: 4, of which 3 were waited for; matrix products, arithmetic and copies ran while one was open for 2% of the time, Pallas kernels for 0%

profile of v5, /device:TPU:0, one launch (start us, length us, event | category | flops | bytes accessed | tf_op | source)
XLA Modules:
  0.0 55.2 jit_solution(11686018600246607457)
XLA Ops:
  0.0 0.0 copy-start
  1.4 0.8 %select_reduce_fusion = s32[8]{0:T(128)S(1)} fusion(s32[8]{0:T(128)} %bitcast.62, s32[8]{0:T(128)} %bitcast.63, pred[8]{0:T(512)(128)(4,1)S(1)} %iota_compare_fusion.3), kind=kLoop, calls=%fused_computation.46 | loop fusion | flops 248 | bytes 104 | tf_op jit(solution)/shard_map/reduce_max | solution.py:110
  2.2 0.1 select_convert_fusion
  2.3 0.0 copy-start.3
  2.3 2.0 %pad_maximum_fusion.1 = bf16[8,8,4736]{2,1,0:T(8,128)(2,1)} fusion(bf16[8,8,128]{2,1,0:T(8,128)(2,1)S(1)} %broadcast_in_dim.76, bf16[8,8,512]{2,1,0:T(8,128)(2,1)} %bitcast.61, bf16[8,8,4096]{2,1,0:T(8,128)(2,1)} %bitcast.56), kind=kLoop, calls=%fused_computation.12 | loop fusion | flops 1818624 | bytes 1212416 | tf_op jit(solution)/shard_map/concatenate | solution.py:142
  4.3 7.3 %all-to-all-start = ((bf16[8,8,4736]{2,1,0:T(8,128)(2,1)}), bf16[8,8,4736]{2,1,0:T(8,128)(2,1)S(1)}, u32[]{:S(2)}, u32[]{:S(2)}) async-start(bf16[8,8,4736]{2,1,0:T(8,128)(2,1)} %pad_maximum_fusion.1), calls=%async_computation | async-start | bytes 1212416 | tf_op jit(solution)/shard_map/all_to_all | solution.py:143
  11.6 16.2 %all-to-all-done = bf16[8,8,4736]{2,1,0:T(8,128)(2,1)S(1)} async-done(((bf16[8,8,4736]{2,1,0:T(8,128)(2,1)}), bf16[8,8,4736]{2,1,0:T(8,128)(2,1)S(1)}, u32[]{:S(2)}, u32[]{:S(2)}) %all-to-all-start) | async-done | bytes 606240 | tf_op jit(solution)/shard_map/all_to_all | solution.py:143
  27.8 0.1 copy.41
  27.9 0.0 copy-done.3
  27.9 0.6 %gather_fusion.1 = bf16[8,32,256]{2,1,0:T(8,128)(2,1)S(1)} fusion(bf16[16,32,256]{2,1,0:T(8,128)(2,1)S(1)} %copy-done.3, s32[1024]{0:T(1024)S(1)} %get-tuple-element.22), kind=kCustom, calls=%fused_computation.1 | custom fusion | bytes 262176 | tf_op jit(solution)/shard_map/jit(_take)/gather | solution.py:151
  28.6 0.6 %gather_fusion = bf16[8,8,4608]{2,1,0:T(8,128)(2,1)S(1)} fusion(bf16[8,8,4608]{2,1,0:T(8,128)(2,1)S(1)} %slice.64, s32[1024]{0:T(1024)S(1)} %get-tuple-element.23), kind=kCustom, calls=%fused_computation | custom fusion | bytes 1179680 | tf_op jit(solution)/shard_map/jit(_take)/gather | solution.py:150
  29.2 0.0 copy-start.1
  29.2 0.9 %pad_maximum_fusion = bf16[8,8,5120]{2,1,0:T(8,128)(2,1)} fusion(bf16[8,8,512]{2,1,0:T(8,128)(2,1)S(1)} %reshape.93, bf16[8,8,4608]{2,1,0:T(8,128)(2,1)S(1)} %gather_fusion), kind=kLoop, calls=%fused_computation.11 | loop fusion | flops 1310720 | bytes 1310720 | tf_op jit(solution)/shard_map/concatenate | solution.py:155
  30.1 3.6 %all-to-all-start.1 = ((bf16[8,8,5120]{2,1,0:T(8,128)(2,1)}), bf16[8,8,5120]{2,1,0:T(8,128)(2,1)S(1)}, u32[]{:S(2)}, u32[]{:S(2)}) async-start(bf16[8,8,5120]{2,1,0:T(8,128)(2,1)} %pad_maximum_fusion), calls=%async_computation.1 | async-start | bytes 1310720 | tf_op jit(solution)/shard_map/all_to_all | solution.py:156
  33.7 0.1 broadcast_in_dim.47
  33.8 0.1 reshape.119
  33.9 0.0 copy-done.1
  34.0 0.3 multiply_cosine_fusion
  34.3 0.1 fusion.13
  34.4 0.1 fusion.12
  34.5 0.0 copy-start.2
  34.5 16.7 %all-to-all-done.1 = bf16[8,8,5120]{2,1,0:T(8,128)(2,1)S(1)} async-done(((bf16[8,8,5120]{2,1,0:T(8,128)(2,1)}), bf16[8,8,5120]{2,1,0:T(8,128)(2,1)S(1)}, u32[]{:S(2)}, u32[]{:S(2)}) %all-to-all-start.1) | async-done | bytes 655392 | tf_op jit(solution)/shard_map/all_to_all | solution.py:156
  51.2 0.0 copy-done
  51.2 0.5 convolution_bitcast_fusion
  51.7 0.1 collective-permute-start
  51.8 0.1 pad_add_fusion
  51.9 0.6 %collective-permute-start.1 = (bf16[8,16,256]{2,1,0:T(8,128)(2,1)S(1)}, bf16[8,16,256]{2,1,0:T(8,128)(2,1)S(1)}, u32[]{:S(2)}, u32[]{:S(2)}) collective-permute-start(bf16[8,16,256]{2,1,0:T(8,128)(2,1)S(1)} %reshape.98), channel_id=1, source_target_pairs={{0,1},{1,0},{2,3},{3,2},{4,5},{5,4},{6,7},{7,6},{8,9},{9,8},{10,11... | collective-permute-start | bytes 196616 | tf_op jit(solution)/shard_map/ppermute | solution.py:161
  52.5 0.5 collective-permute-done
  53.0 0.0 copy-done.2
  53.0 0.2 fusion.1
  53.2 0.1 slice_negate_fusion
  53.4 0.1 fusion.4
  53.5 0.0 collective-permute-done.1
  53.6 0.2 tile.4
  53.7 0.3 fusion.19
  54.0 0.2 fusion.2
  54.2 0.3 convolution_convert_fusion
  54.5 0.7 %copy.51 = bf16[4,16,8,128]{3,2,0,1:T(8,128)(2,1)} copy(bf16[4,16,8,128]{3,2,1,0:T(8,128)(2,1)S(1)} %bitcast.59) | data formatting | bytes 262144 | tf_op jit(solution)/shard_map/reshape | solution.py:80
  (23 shorter events, 0.3 us)
Async XLA Ops:
  0.0 51.2 %copy-start = (bf16[128,4096]{1,0:T(8,128)(2,1)S(1)}, bf16[128,4096]{1,0:T(8,128)(2,1)}, u32[]{:S(2)}) copy-start(bf16[128,4096]{1,0:T(8,128)(2,1)} %param.10) | copy-start | bytes 3145732
  2.3 25.6 %copy-start.3 = (bf16[16,32,256]{2,1,0:T(8,128)(2,1)S(1)}, bf16[16,32,256]{2,1,0:T(8,128)(2,1)}, u32[]{:S(2)}) copy-start(bf16[16,32,256]{2,1,0:T(8,128)(2,1)} %param.13) | copy-start | bytes 786436
  4.3 23.5 %all-to-all-start = ((bf16[8,8,4736]{2,1,0:T(8,128)(2,1)}), bf16[8,8,4736]{2,1,0:T(8,128)(2,1)S(1)}, u32[]{:S(2)}, u32[]{:S(2)}) async-start(bf16[8,8,4736]{2,1,0:T(8,128)(2,1)} %pad_maximum_fusion.1), calls=%async_computation | async-start | bytes 1212416 | tf_op jit(solution)/shard_map/all_to_all | solution.py:143
  29.2 4.8 %copy-start.1 = (bf16[128,256]{1,0:T(8,128)(2,1)S(1)}, bf16[128,256]{1,0:T(8,128)(2,1)}, u32[]{:S(2)}) copy-start(bf16[128,256]{1,0:T(8,128)(2,1)} %param.12) | copy-start | bytes 196612
  30.1 21.1 %all-to-all-start.1 = ((bf16[8,8,5120]{2,1,0:T(8,128)(2,1)}), bf16[8,8,5120]{2,1,0:T(8,128)(2,1)S(1)}, u32[]{:S(2)}, u32[]{:S(2)}) async-start(bf16[8,8,5120]{2,1,0:T(8,128)(2,1)} %pad_maximum_fusion), calls=%async_computation.1 | async-start | bytes 1310720 | tf_op jit(solution)/shard_map/all_to_all | solution.py:156
  34.5 18.5 %copy-start.2 = (bf16[128,512]{1,0:T(8,128)(2,1)S(1)}, bf16[128,512]{1,0:T(8,128)(2,1)}, u32[]{:S(2)}) copy-start(bf16[128,512]{1,0:T(8,128)(2,1)} %param.11) | copy-start | bytes 393220
  51.7 1.3 %collective-permute-start = (f32[128,64]{0,1:T(8,128)S(1)}, f32[128,64]{0,1:T(8,128)S(1)}, u32[]{:S(2)}, u32[]{:S(2)}) collective-permute-start(f32[128,64]{0,1:T(8,128)S(1)} %convolution_bitcast_fusion), channel_id=1, source_target_pairs={{0,1},{1,0},{2,3},{3,2},{4,5},{5,4},{6,7},{7,6},{8,9},{9,8},{10,11... | collective-permute-start | bytes 98312 | tf_op jit(solution)/shard_map/ppermute | solution.py:194
  51.9 1.6 %collective-permute-start.1 = (bf16[8,16,256]{2,1,0:T(8,128)(2,1)S(1)}, bf16[8,16,256]{2,1,0:T(8,128)(2,1)S(1)}, u32[]{:S(2)}, u32[]{:S(2)}) collective-permute-start(bf16[8,16,256]{2,1,0:T(8,128)(2,1)S(1)} %reshape.98), channel_id=1, source_target_pairs={{0,1},{1,0},{2,3},{3,2},{4,5},{5,4},{6,7},{7,6},{8,9},{9,8},{10,11... | collective-permute-start | bytes 196616 | tf_op jit(solution)/shard_map/ppermute | solution.py:161
